TPU v7x, 256 devices: a whole 4x4x8 slice. The times are simulated.
256 devices in a mesh: row: 32 (over y_hi, z, core), col: 8 (over y_lo, x).
Axes of the slice: x: 4, y: 4 (y_hi: 2, y_lo: 2; y = y_hi * 2 + y_lo), z: 8, core: 2. Of those that a mesh axis runs over, the one named last changes fastest.
Arguments:
- colloc: bfloat16 [2, 2048, 9216], P(None, 'row'), may hold values from -6 to 6
- coefficients: bfloat16 [2, 9216, 512], P(None, 'row'), may hold values from -0.0625 to 0.0625
- occupied: int32 [2], replicated, may hold values from 256 to 512
- offsets: int32 [2, 2], replicated, may hold values from 0 to 2048
Outputs:
- exchange_matrix: bfloat16 [9216, 2, 9216], P('col', None, 'row')
Inputs may be any that keep to these rules, and one draw needn't show every extreme that they name: occupied[s] is the number of occupied orbitals of spin s. offsets[s, k] is the first point of panel k of spin s on the line of 73728 points; both panels lie within the first 3072 points and may intersect.
All inputs are finite; a program needn't handle non-finite values.
Results may differ from a plain program's by a relative error of at most 0.019.
Values may be sent and summed in bfloat16 or wider, within the bound.
No kernel may reach another device: no remote copies, remote signals or barrier semaphores. Data moves between devices by JAX's collectives and lax.ppermute only.
A program may use at most 128 MiB of HBM per device.

v0:
```python
import math

import jax
import jax.numpy as jnp
from jax import lax
from jax.sharding import PartitionSpec as P


def point_positions(point_ids, offsets, panel_len):
    first = jnp.where(point_ids[None, :] // panel_len == 0, offsets[:, 0:1], offsets[:, 1:2])
    return (first + point_ids[None, :] % panel_len).astype(jnp.float32)


def local(colloc, coefficients, occupied, offsets):
    row_count = lax.axis_size("row")
    col_count = lax.axis_size("col")
    col_index = lax.axis_index("col")
    spin_count, own_points, basis = colloc.shape
    slots = coefficients.shape[2]
    sub_rows = own_points // col_count
    group_points = row_count * sub_rows
    points = own_points * row_count
    panel_len = points // 2
    screen_len = panel_len // 8
    norm_factor = 1.0 / math.sqrt(points)
    own_rows = lax.dynamic_slice_in_dim(colloc, col_index * sub_rows, sub_rows, 1)
    regrouped = lax.all_to_all(own_rows, "row", split_axis=2, concat_axis=1, tiled=True)
    partial_value = jnp.einsum(
        "spm,smi->spi", regrouped, coefficients, preferred_element_type=jnp.float32
    )
    summed = lax.psum(partial_value, "row")
    occupied_mask = jnp.arange(slots, dtype=jnp.int32)[None, :] < occupied[:, None]
    orbitals_own = jnp.where(occupied_mask[:, None, :], summed, 0.0).astype(jnp.bfloat16)
    orbitals_all, basis_all = (
        lax.all_gather(orbitals_own, "col", axis=1, tiled=True),
        lax.all_gather(regrouped, "col", axis=1, tiled=True),
    )
    local_ids = jnp.arange(group_points, dtype=jnp.int32)
    own_ids = local_ids // sub_rows * own_points + col_index * sub_rows + local_ids % sub_rows
    every_ids = jnp.arange(points, dtype=jnp.int32)
    every_group = every_ids // group_points
    every_rest = every_ids % group_points
    all_ids = every_rest // sub_rows * own_points + every_group * sub_rows + every_rest % sub_rows
    own_positions = point_positions(own_ids, offsets, panel_len)
    all_positions = point_positions(all_ids, offsets, panel_len)
    kernel = 1.0 / (
        1.0 + jnp.abs(own_positions[:, :, None] - all_positions[:, None, :]) / screen_len
    )
    density = jnp.einsum(
        "spi,sqi->spq", orbitals_own, orbitals_all, preferred_element_type=jnp.float32
    )
    mixed_kernel = (kernel * density / slots).astype(jnp.bfloat16)
    weighted = jnp.einsum(
        "spq,sqn->spn", mixed_kernel, basis_all, preferred_element_type=jnp.float32
    ).astype(jnp.bfloat16)
    basis_rows = lax.all_gather(own_rows, "row", axis=1, tiled=True)
    return lax.psum_scatter(
        (
            jnp.einsum("spm,spn->msn", basis_rows, weighted, preferred_element_type=jnp.float32)
            * norm_factor
        ).astype(jnp.bfloat16),
        "col",
        scatter_dimension=0,
        tiled=True,
    )


def solution(mesh):
    placed = (P(None, "row", None), P(None, "row", None), P(), P())
    return jax.shard_map(
        local, mesh=mesh, in_specs=placed, out_specs=P("col", None, "row"), check_vma=False
    )
```

profile of v0, /device:TPU:1, one launch (start us, length us, event | category | flops | bytes accessed | tf_op | source)
XLA Modules:
  0.0 533.7 jit_solution(1746210762000152768)
XLA Ops:
  6.5 1.7 copy-done
  8.2 7.7 %copy.8 = bf16[2,8,9216]{1,0,2:T(2,128)(2,1)} copy(bf16[2,8,9216]{2,1,0:T(8,128)(2,1)S(1)} %constant_dynamic-slice_fusion) | data formatting | bytes 589824 | tf_op jit(solution)/shard_map/dynamic_slice | solution.py:26
  15.9 13.6 %reshape.310 = bf16[32,2,2304]{2,1,0:T(2,128)(2,1)S(1)} reshape(bf16[9216,2,8]{2,1,0:T(2,128)(2,1)} %bitcast.21) | data formatting | bytes 589824
  29.5 26.6 %all_to_all.18 = bf16[32,2,2304]{2,1,0:T(2,128)(2,1)S(1)} all-to-all(bf16[32,2,2304]{2,1,0:T(2,128)(2,1)S(1)} %reshape.310), channel_id=1, replica_groups=mesh['row'=32,'col'=8] {'row'}, dimensions={0} | all-to-all | bytes 589824 | tf_op jit(solution)/shard_map/all_to_all | solution.py:27
  56.1 6.6 %reshape.311 = bf16[9216,2,8]{2,1,0:T(2,128)(2,1)} reshape(bf16[32,2,2304]{2,1,0:T(2,128)(2,1)S(1)} %all_to_all.18) | data formatting | bytes 589824
  62.7 9.3 %copy.9 = bf16[2,8,32,288]{3,1,2,0:T(8,128)(2,1)S(1)} copy(bf16[2,8,32,288]{1,0,3,2:T(2,128)(2,1)} %bitcast.20) | data formatting | bytes 589824 | tf_op jit(solution)/shard_map/all_to_all | solution.py:27
  72.0 0.9 copy.11
  73.0 0.0 all-gather.4.cloned.1.call-start
  73.0 0.1 iota_compare_fusion
  73.1 1.6 fusion.27
  74.7 136.9 %all-reduce.1 = bf16[2,256,512]{2,1,0:T(8,128)(2,1)} all-reduce(f32[2,256,512]{2,1,0:T(8,128)S(1)} %fusion.27), channel_id=1, replica_groups=mesh['row'=32,'col'=8] {'row'}, use_global_device_ids=true, to_apply=%region_0.0 | all-reduce | flops 262144 | bytes 1572864 | tf_op jit(solution)/shard_map/psum | solution.py:31
  211.6 1.9 select_convert_fusion
  213.6 0.0 all-gather.8.cloned.1.call-start
  213.6 0.7 all-gather.8.cloned.1.call-update
  214.4 0.2 slice_reduce_fusion.1
  214.6 0.1 add_convert_fusion.1
  214.7 0.1 add_convert_fusion
  214.8 53.4 %all-gather.4.cloned.1.call-done = bf16[2,2048,512]{2,1,0:T(8,128)(2,1)} async-done(((bf16[2,256,512]{2,1,0:T(8,128)(2,1)}), bf16[2,2048,512]{2,1,0:T(8,128)(2,1)}) %all-gather.4.cloned.1.call-update) | async-done | bytes 4194320 | tf_op jit(solution)/shard_map/all_gather | solution.py:35
  268.2 5.3 convolution_convert_fusion
  273.4 101.8 %all-gather.8.cloned.1.call-done = bf16[2,256,9216]{2,1,0:T(8,128)(2,1)} async-done(((bf16[2,8,9216]{2,1,0:T(8,128)(2,1)}), bf16[2,256,9216]{2,1,0:T(8,128)(2,1)}) %all-gather.8.cloned.1.call-update) | async-done | bytes 9437200 | tf_op jit(solution)/shard_map/all_gather | solution.py:56
  375.2 9.8 %multiply_convert_fusion = bf16[2,288,9216]{2,1,0:T(8,128)(2,1)} fusion(bf16[2,256,288]{1,2,0:T(8,128)(2,1)S(1)} %convolution_convert_fusion, bf16[2,256,9216]{2,1,0:T(8,128)(2,1)} %all-gather.8.cloned.1.call-done), kind=kOutput, calls=%fused_computation | convolution fusion | flops 2728525824 | bytes 20348928 | tf_op jit(solution)/shard_map/spm,spn->msn/dot_general | solution.py:59
  385.0 15.6 %copy.15 = bf16[9216,576]{1,0:T(8,128)(2,1)} copy(bf16[9216,576]{0,1:T(8,128)(2,1)} %bitcast.19) | data formatting | bytes 21233664
  400.7 123.9 %reduce-scatter.4.cloned.1.call-done = bf16[1152,576]{1,0:T(8,128)(2,1)} async-done(((bf16[9216,576]{1,0:T(8,128)(2,1)}), bf16[1152,576]{1,0:T(8,128)(2,1)}) %reduce-scatter.4.cloned.1.call-update) | async-done | bytes 1327120
  524.6 2.6 copy.16
  (20 shorter events, 0.2 us)
Async XLA Ops:
  6.5 1.7 copy-start
  6.5 208.3 %all-gather.6.cloned.1.call-start = ((), (), s32[]{:S(2)}) async-start(), calls=%async_computation.3 | async-start | bytes 2654208 | tf_op jit(solution)/shard_map/all_gather | solution.py:36
  8.2 21.3 %copy-start.2 = (bf16[2,8,9216]{2,1,0:T(8,128)(2,1)}, bf16[2,8,9216]{2,1,0:T(8,128)(2,1)S(1)}, u32[]{:S(2)}) copy-start(bf16[2,8,9216]{2,1,0:T(8,128)(2,1)S(1)} %constant_dynamic-slice_fusion) | copy-start | bytes 884740
  62.7 10.4 %copy-start.4 = (s32[2]{0:T(128)S(1)}, s32[2]{0:T(128)}, u32[]{:S(2)}) copy-start(s32[2]{0:T(128)} %param.6) | copy-start | bytes 28
  72.0 1.0 copy-start.1
  72.0 142.4 %copy-start.3 = (s32[2,2]{1,0:T(2,128)S(1)}, s32[2,2]{1,0:T(2,128)}, u32[]{:S(2)}) copy-start(s32[2,2]{1,0:T(2,128)} %param.7) | copy-start | bytes 52
  73.0 195.2 %all-gather.4.cloned.1.call-start = ((), (), s32[]{:S(2)}) async-start(), calls=%async_computation.2 | async-start | bytes 4718592 | tf_op jit(solution)/shard_map/all_gather | solution.py:35
  213.6 161.6 %all-gather.8.cloned.1.call-start = ((), (), s32[]{:S(2)}) async-start(), calls=%async_computation.4 | async-start | bytes 9732096 | tf_op jit(solution)/shard_map/all_gather | solution.py:56
  214.3 310.3 %reduce-scatter.4.cloned.1.call-start = ((), (), s32[]{:S(2)}) async-start(), calls=%async_computation.5 | async-start | bytes 13271040
Sparse Core Ops, SparseCore 0:
  73.1 40.1 all-gather.5
  213.7 54.4 all-gather.3
  271.0 104.1 all-gather.7
  400.8 123.7 reduce-scatter.3
where the time goes:
time: 535 us; the launch traced here: 534 us
  waiting for transfers between devices  280 us (52%)
  blocking collectives  163 us (30%)
  local copies, waits for them, and re-layouts  58.2 us (11%)
  matrix products  16.7 us (3%)
  between operations  13.2 us (2%)
    psum x1, blocking collectives, local(): summed = lax.psum(partial_value, 'row')  137 us
    unnamed x5, waiting for transfers between devices  125 us
    all_gather x1, waiting for transfers between devices, local(): basis_rows = lax.all_gather(own_rows, 'row', axis=1, tiled=True)  102 us
    all_gather x1, waiting for transfers between devices, local(): lax.all_gather(orbitals_own, 'col', axis=1, tiled=True)  53.4 us
    unnamed x14, local copies, waits for them, and re-layouts  40 us
    all_to_all x1, blocking collectives, local(): lax.all_to_all(own_rows, 'row', split_axis=2, concat_axis=1, tiled=True)  26.6 us
  transfers between devices with their start and end apart: 4, of which 3 were waited for; matrix products, arithmetic and copies ran while one was open for 2% of the time, Pallas kernels for 0%

commit v1 on v0

v1 whole, which is shorter than its diff:
```python
import math

import jax
import jax.numpy as jnp
from jax import lax
from jax.sharding import PartitionSpec as P


def point_positions(point_ids, offsets, panel_len):
    first = jnp.where(point_ids[None, :] // panel_len == 0, offsets[:, 0:1], offsets[:, 1:2])
    return (first + point_ids[None, :] % panel_len).astype(jnp.float32)


def local(colloc, coefficients, occupied, offsets):
    row_count = lax.axis_size("row")
    col_count = lax.axis_size("col")
    col_index = lax.axis_index("col")
    spin_count, own_points, basis = colloc.shape
    slots = coefficients.shape[2]
    sub_rows = own_points // col_count
    points = own_points * row_count
    panel_len = points // 2
    screen_len = panel_len // 8
    col_width = basis // col_count
    norm_factor = 1.0 / math.sqrt(points)

    own_cols = lax.dynamic_slice_in_dim(colloc, col_index * col_width, col_width, 2)
    basis_cols = lax.all_gather(own_cols, "row", axis=1, tiled=True)

    own_rows = lax.dynamic_slice_in_dim(colloc, col_index * sub_rows, sub_rows, 1)
    regrouped = lax.all_to_all(own_rows, "row", split_axis=2, concat_axis=1, tiled=True)
    partial_value = jnp.einsum(
        "spm,smi->spi", regrouped, coefficients, preferred_element_type=jnp.float32
    )
    summed = lax.psum_scatter(partial_value, "row", scatter_dimension=1, tiled=True)
    occupied_mask = jnp.arange(slots, dtype=jnp.int32)[None, :] < occupied[:, None]
    orbitals_own = jnp.where(occupied_mask[:, None, :], summed, 0.0).astype(jnp.bfloat16)
    orbitals_all = lax.all_gather(orbitals_own, ("row", "col"), axis=1, tiled=True)

    basis_group = lax.all_gather(regrouped, "col", axis=1, tiled=True)
    basis_rows = (
        basis_group.reshape(spin_count, col_count, row_count, sub_rows, -1)
        .transpose(0, 2, 1, 3, 4)
        .reshape(spin_count, points, -1)
    )

    positions = point_positions(jnp.arange(points, dtype=jnp.int32), offsets, panel_len)
    kernel = 1.0 / (1.0 + jnp.abs(positions[:, :, None] - positions[:, None, :]) / screen_len)
    density = jnp.einsum(
        "spi,sqi->spq", orbitals_all, orbitals_all, preferred_element_type=jnp.float32
    )
    mixed_kernel = (kernel * density / slots).astype(jnp.bfloat16)
    weighted = jnp.einsum(
        "spq,sqn->spn", mixed_kernel, basis_rows, preferred_element_type=jnp.float32
    ).astype(jnp.bfloat16)
    return (
        jnp.einsum("spm,spn->msn", basis_cols, weighted, preferred_element_type=jnp.float32)
        * norm_factor
    ).astype(jnp.bfloat16)


def solution(mesh):
    placed = (P(None, "row", None), P(None, "row", None), P(), P())
    return jax.shard_map(
        local, mesh=mesh, in_specs=placed, out_specs=P("col", None, "row"), check_vma=False
    )
```

time: 535 us -> 1030 us (1.93)
  waiting for transfers between devices: 280 us -> 909 us
  blocking collectives: 163 us -> 26.6 us
  local copies, waits for them, and re-layouts: 58.2 us -> 43.9 us
  matrix products: 16.7 us -> 29.6 us
    all_gather x3, waiting for transfers between devices: 155 us -> 803 us  [the longest x1 715 us: local(): lax.all_gather(orbitals_own, ('row', 'col'), axis=1, tiled=True)]
    psum x1 -> x0, blocking collectives: 137 us -> none  [local(): summed = lax.psum(partial_value, 'row')]
    unnamed x5 -> x4, waiting for transfers between devices: 125 us -> 0.56 us
    reduce_scatter x0 -> x1, waiting for transfers between devices: none -> 105 us  [local(): lax.psum_scatter(partial_value, 'row', scatter_dimension=1, tiled=True)]
    dot_general x2, matrix products: 15.1 us -> 28.2 us  [the longest x1 19.5 us: local(): jnp.einsum('spq,sqn->spn', mixed_kernel, basis_rows, preferred_element_ty...]
    unnamed x14 -> x13, local copies, waits for them, and re-layouts: 40 us -> 29.5 us
  transfers between devices with their start and end apart: 4 -> 4, of which waited for: 3 -> 3; matrix products, arithmetic and copies ran while one was open for 2% -> 3% of each run, Pallas kernels for 0% -> 0%
where the time goes in v1:
time: 1030 us
  waiting for transfers between devices  909 us (88%)
  local copies, waits for them, and re-layouts  43.9 us (4%)
  matrix products  29.6 us (3%)
  blocking collectives  26.6 us (3%)
  between operations  15.1 us (1%)
    all_gather x1, waiting for transfers between devices, local(): lax.all_gather(orbitals_own, ('row', 'col'), axis=1, tiled=True)  715 us
    reduce_scatter x1, waiting for transfers between devices, local(): lax.psum_scatter(partial_value, 'row', scatter_dimension=1, tiled=True)  105 us
    all_gather x1, waiting for transfers between devices, local(): basis_cols = lax.all_gather(own_cols, 'row', axis=1, tiled=True)  87.7 us
    unnamed x13, local copies, waits for them, and re-layouts  29.5 us
    all_to_all x1, blocking collectives, local(): lax.all_to_all(own_rows, 'row', split_axis=2, concat_axis=1, tiled=True)  26.6 us
  transfers between devices with their start and end apart: 4, of which 3 were waited for; matrix products, arithmetic and copies ran while one was open for 3% of the time, Pallas kernels for 0%

profile of v1, /device:TPU:1, one launch (start us, length us, event | category | flops | bytes accessed | tf_op | source)
XLA Modules:
  0.0 1025.7 jit_solution(12236467226483842061)
XLA Ops:
  7.4 1.7 copy-done
  9.1 7.6 copy.14
  16.7 13.6 %reshape.189 = bf16[32,2,2304]{2,1,0:T(2,128)(2,1)S(1)} reshape(bf16[9216,2,8]{2,1,0:T(2,128)(2,1)} %bitcast.28) | data formatting | bytes 589824
  30.3 26.6 %all_to_all.18 = bf16[32,2,2304]{2,1,0:T(2,128)(2,1)S(1)} all-to-all(bf16[32,2,2304]{2,1,0:T(2,128)(2,1)S(1)} %reshape.189), channel_id=1, replica_groups=mesh['row'=32,'col'=8] {'row'}, dimensions={0} | all-to-all | bytes 589824 | tf_op jit(solution)/shard_map/all_to_all | solution.py:31
  56.9 6.6 reshape.190
  63.5 9.4 copy.8
  72.8 1.4 fusion.12
  74.3 0.0 all-gather.6.cloned.1.call-start
  74.3 0.5 all-gather.6.cloned.1.call-update
  74.9 0.0 all-gather.4.cloned.1.call-start
  74.9 0.1 iota_compare_fusion
  75.0 105.1 %reduce-scatter.2.cloned.1.call-done = f32[2,8,512]{2,1,0:T(8,128)} async-done(((f32[2,256,512]{2,1,0:T(8,128)}), f32[2,8,512]{2,1,0:T(8,128)}) %reduce-scatter.2.cloned.1.call-update) | async-done | bytes 32784 | tf_op jit(solution)/shard_map/reduce_scatter | solution.py:35
  180.1 1.4 select_convert_fusion
  181.5 0.0 all-gather.4.cloned.1.call-update
  181.5 0.2 all-gather.8.cloned.1.call-start
  181.7 0.7 constant_dynamic-slice_fusion
  182.5 0.2 slice_reduce_fusion.1
  182.7 0.1 add_convert_fusion
  182.8 0.0 all-gather.6.cloned.1.call-done
  182.8 4.1 copy.10
  186.9 715.2 %all-gather.4.cloned.1.call-done = bf16[2,2048,512]{2,1,0:T(8,128)(2,1)} async-done(((bf16[2,8,512]{2,1,0:T(8,128)(2,1)}), bf16[2,2048,512]{2,1,0:T(8,128)(2,1)}) %all-gather.4.cloned.1.call-update) | async-done | bytes 4194320 | tf_op jit(solution)/shard_map/all_gather | solution.py:38
  902.2 19.5 %fusion.1 = bf16[2,2048,288]{1,2,0:T(8,128)(2,1)} fusion(bf16[2,2048,288]{2,1,0:T(8,128)(2,1)} %bitcast.32, f32[2,2048]{1,0:T(2,128)S(1)} %add_convert_fusion, bf16[2,2048,512]{2,1,0:T(8,128)(2,1)} %all-gather.4.cloned.1.call-done), kind=kOutput, calls=%fused_computation.3 | convolution fusion | flops 13490061312 | bytes 8929280 | tf_op jit(solution)/shard_map/spq,sqn->spn/dot_general | solution.py:53
  921.7 87.7 %all-gather.8.cloned.1.call-done = bf16[2,2048,1152]{2,1,0:T(8,128)(2,1)} async-done(((bf16[2,64,1152]{2,1,0:T(8,128)(2,1)}), bf16[2,2048,1152]{2,1,0:T(8,128)(2,1)}) %all-gather.8.cloned.1.call-update) | async-done | bytes 9437200 | tf_op jit(solution)/shard_map/all_gather | solution.py:28
  1009.4 8.7 fusion.3
  (15 shorter events, 0.1 us)
Async XLA Ops:
  7.4 1.7 copy-start
  7.4 172.8 %reduce-scatter.2.cloned.1.call-start = ((), (), s32[]{:S(2)}) async-start(), calls=%async_computation.2 | async-start | bytes 1081344 | tf_op jit(solution)/shard_map/reduce_scatter | solution.py:35
  56.9 15.9 %copy-start.2 = (bf16[2,288,512]{2,1,0:T(8,128)(2,1)S(1)}, bf16[2,288,512]{2,1,0:T(8,128)(2,1)}, u32[]{:S(2)}) copy-start(bf16[2,288,512]{2,1,0:T(8,128)(2,1)} %param.5) | copy-start | bytes 1769476
  63.5 11.4 %copy-start.4 = (s32[2]{0:T(128)S(1)}, s32[2]{0:T(128)}, u32[]{:S(2)}) copy-start(s32[2]{0:T(128)} %param.6) | copy-start | bytes 28
  63.5 119.1 %copy-start.3 = (s32[2,2]{1,0:T(2,128)S(1)}, s32[2,2]{1,0:T(2,128)}, u32[]{:S(2)}) copy-start(s32[2,2]{1,0:T(2,128)} %param.7) | copy-start | bytes 52
  72.8 1.5 copy-start.1
  74.3 108.6 %all-gather.6.cloned.1.call-start = ((), (), s32[]{:S(2)}) async-start(), calls=%async_computation.4 | async-start | bytes 3538944 | tf_op jit(solution)/shard_map/all_gather | solution.py:40
  74.9 827.3 %all-gather.4.cloned.1.call-start = ((), (), s32[]{:S(2)}) async-start(), calls=%async_computation.3 | async-start | bytes 4210688 | tf_op jit(solution)/shard_map/all_gather | solution.py:38
  181.5 827.9 %all-gather.8.cloned.1.call-start = ((), (), s32[]{:S(2)}) async-start(), calls=%async_computation.5 | async-start | bytes 9732096 | tf_op jit(solution)/shard_map/all_gather | solution.py:28
Sparse Core Ops, SparseCore 0:
  74.4 105.6 reduce-scatter.1
Sparse Core Ops, SparseCore 1:
  76.5 38.9 all-gather.5
  181.6 720.5 all-gather.3
  904.9 104.5 all-gather.7

commit v2 on v1

v2 whole, which is shorter than its diff:
```python
import math

import jax
import jax.numpy as jnp
from jax import lax
from jax.sharding import PartitionSpec as P


def point_positions(point_ids, offsets, panel_len):
    first = jnp.where(point_ids[None, :] // panel_len == 0, offsets[:, 0:1], offsets[:, 1:2])
    return (first + point_ids[None, :] % panel_len).astype(jnp.float32)


def local(colloc, coefficients, occupied, offsets):
    row_count = lax.axis_size("row")
    col_count = lax.axis_size("col")
    col_index = lax.axis_index("col")
    spin_count, own_points, basis = colloc.shape
    slots = coefficients.shape[2]
    sub_rows = own_points // col_count
    points = own_points * row_count
    panel_len = points // 2
    screen_len = panel_len // 8
    col_width = basis // col_count
    row_width = basis // row_count
    norm_factor = 1.0 / math.sqrt(points)

    own_cols = lax.dynamic_slice_in_dim(colloc, col_index * col_width, col_width, 2)
    basis_cols = lax.all_gather(own_cols, "row", axis=1, tiled=True)

    own_rows = lax.dynamic_slice_in_dim(colloc, col_index * sub_rows, sub_rows, 1)
    send = own_rows.reshape(spin_count, sub_rows, row_count, row_width).transpose(2, 0, 1, 3)
    regrouped = lax.all_to_all(send, "row", split_axis=0, concat_axis=0, tiled=True)
    basis_all = lax.all_gather(regrouped, "col", axis=0)

    partial_value = jnp.einsum(
        "xspm,smi->xspi", regrouped, coefficients, preferred_element_type=jnp.float32
    )
    received = lax.all_to_all(partial_value, "row", split_axis=0, concat_axis=0, tiled=True)
    summed = jnp.sum(received, axis=0)
    occupied_mask = jnp.arange(slots, dtype=jnp.int32)[None, :] < occupied[:, None]
    orbitals_own = jnp.where(occupied_mask[:, None, :], summed, 0.0).astype(jnp.bfloat16)
    spread = jnp.broadcast_to(orbitals_own[None], (row_count,) + orbitals_own.shape)
    orbitals_group = lax.all_to_all(spread, "row", split_axis=0, concat_axis=0, tiled=True)
    orbitals_all = lax.all_gather(orbitals_group, "col", axis=0)

    def flat(x):
        return jnp.moveaxis(x, 2, 0).reshape(spin_count, points, x.shape[-1])

    orbitals_perm = flat(orbitals_all)
    basis_perm = flat(basis_all)
    ids = jnp.arange(points, dtype=jnp.int32)
    group_of, rest = ids // (row_count * sub_rows), ids % (row_count * sub_rows)
    perm_ids = rest // sub_rows * own_points + group_of * sub_rows + rest % sub_rows
    positions = point_positions(perm_ids, offsets, panel_len)
    kernel = 1.0 / (1.0 + jnp.abs(positions[:, :, None] - positions[:, None, :]) / screen_len)
    density = jnp.einsum(
        "spi,sqi->spq", orbitals_perm, orbitals_perm, preferred_element_type=jnp.float32
    )
    mixed_kernel = (kernel * density / slots).astype(jnp.bfloat16)
    weighted = jnp.einsum(
        "spq,sqn->spn", mixed_kernel, basis_perm, preferred_element_type=jnp.float32
    ).astype(jnp.bfloat16)
    weighted = (
        weighted.reshape(spin_count, col_count, row_count, sub_rows, -1)
        .transpose(0, 2, 1, 3, 4)
        .reshape(spin_count, points, -1)
    )
    return (
        jnp.einsum("spm,spn->msn", basis_cols, weighted, preferred_element_type=jnp.float32)
        * norm_factor
    ).astype(jnp.bfloat16)


def solution(mesh):
    placed = (P(None, "row", None), P(None, "row", None), P(), P())
    return jax.shard_map(
        local, mesh=mesh, in_specs=placed, out_specs=P("col", None, "row"), check_vma=False
    )
```

time: 1030 us -> 288 us (0.28)
  waiting for transfers between devices: 909 us -> 156 us
  local copies, waits for them, and re-layouts: 43.9 us -> 12.6 us
  blocking collectives: 26.6 us -> 53.5 us
  matrix products: 29.6 us -> 46.8 us
    all_gather x2, waiting for transfers between devices: 715 us -> 45.7 us  [the longest x1 45.7 us: local(): orbitals_all = lax.all_gather(orbitals_group, 'col', axis=0)]
    reduce_scatter x1 -> x0, waiting for transfers between devices: 105 us -> none  [local(): lax.psum_scatter(partial_value, 'row', scatter_dimension=1, tiled=True)]
    all_to_all x0 -> x1, waiting for transfers between devices: none -> 44.8 us  [local(): lax.all_to_all(partial_value, 'row', split_axis=0, concat_axis=0, tiled=T...]
    unnamed x13 -> x8, local copies, waits for them, and re-layouts: 29.5 us -> 1.68 us
    all_to_all x1 -> x2, blocking collectives: 26.6 us -> 53.5 us  [the longest x1 28.2 us: local(): lax.all_to_all(send, 'row', split_axis=0, concat_axis=0, tiled=True)]
    all_gather x1, waiting for transfers between devices: 87.7 us -> 65.3 us  [local(): basis_cols = lax.all_gather(own_cols, 'row', axis=1, tiled=True)]
    dot_general x2 -> x3, matrix products: 20.9 us -> 37.6 us  [the longest x1 18.9 us: local(): jnp.einsum('spi,sqi->spq', orbitals_perm, orbitals_perm, preferred_elemen...]
  transfers between devices with their start and end apart: 4 -> 4, of which waited for: 3 -> 3; matrix products, arithmetic and copies ran while one was open for 3% -> 17% of each run, Pallas kernels for 0% -> 0%
where the time goes in v2:
time: 288 us
  waiting for transfers between devices  156 us (54%)
  blocking collectives  53.5 us (19%)
  matrix products  46.8 us (16%)
  between operations  13.2 us (5%)
  local copies, waits for them, and re-layouts  12.6 us (4%)
  starting transfers between devices  5.87 us (2%)
    all_gather x1, waiting for transfers between devices, local(): basis_cols = lax.all_gather(own_cols, 'row', axis=1, tiled=True)  65.3 us
    all_gather x1, waiting for transfers between devices, local(): orbitals_all = lax.all_gather(orbitals_group, 'col', axis=0)  45.7 us
    all_to_all x1, waiting for transfers between devices, local(): lax.all_to_all(partial_value, 'row', split_axis=0, concat_axis=0, tiled=T...  44.8 us
    all_to_all x1, blocking collectives, local(): lax.all_to_all(send, 'row', split_axis=0, concat_axis=0, tiled=True)  28.2 us
    all_to_all x1, blocking collectives, local(): lax.all_to_all(spread, 'row', split_axis=0, concat_axis=0, tiled=True)  25.3 us
    dot_general x1, matrix products, local(): jnp.einsum('spi,sqi->spq', orbitals_perm, orbitals_perm, preferred_elemen...  18.9 us
    dot_general x1, matrix products, local(): jnp.einsum('spq,sqn->spn', mixed_kernel, basis_perm, preferred_element_ty...  17.1 us
    dot_general x1, matrix products, local(): jnp.einsum('spm,spn->msn', basis_cols, weighted, preferred_element_type=j...  9.13 us
  transfers between devices with their start and end apart: 4, of which 3 were waited for; matrix products, arithmetic and copies ran while one was open for 17% of the time, Pallas kernels for 0%

profile of v2, /device:TPU:1, one launch (start us, length us, event | category | flops | bytes accessed | tf_op | source)
XLA Modules:
  0.0 288.1 jit_solution(8310522475610055564)
XLA Ops:
  6.5 1.7 copy-done
  8.2 0.6 reshape.248
  8.9 0.1 copy.21
  9.0 28.2 %all_to_all.15 = bf16[32,2,8,288]{3,2,1,0:T(8,128)(2,1)} all-to-all(bf16[32,2,8,288]{3,2,1,0:T(8,128)(2,1)S(1)} %copy.21), channel_id=1, replica_groups=mesh['row'=32,'col'=8] {'row'}, dimensions={0} | all-to-all | bytes 589824 | tf_op jit(solution)/shard_map/all_to_all | solution.py:33
  37.2 1.6 convolution_bitcast_fusion
  38.9 1.1 copy.23
  39.9 5.6 %all-to-all-start.1 = ((f32[32,2,8,512]{3,2,1,0:T(8,128)}), f32[32,2,8,512]{3,2,1,0:T(8,128)S(1)}, u32[]{:S(2)}, u32[]{:S(2)}) async-start(f32[32,2,8,512]{3,2,1,0:T(8,128)} %copy.23), calls=%async_computation.1 | async-start | bytes 2097152 | tf_op jit(solution)/shard_map/all_to_all | solution.py:39
  45.6 0.1 iota_compare_fusion
  45.7 44.8 %all-to-all-done.1 = f32[32,2,8,512]{3,2,1,0:T(8,128)S(1)} async-done(((f32[32,2,8,512]{3,2,1,0:T(8,128)}), f32[32,2,8,512]{3,2,1,0:T(8,128)S(1)}, u32[]{:S(2)}, u32[]{:S(2)}) %all-to-all-start.1) | async-done | bytes 1048608 | tf_op jit(solution)/shard_map/all_to_all | solution.py:39
  90.5 0.1 reduce_sum.9
  90.6 0.1 broadcast_in_dim.54
  90.6 25.3 %all_to_all.16 = bf16[32,2,8,512]{3,2,1,0:T(8,128)(2,1)} all-to-all(bf16[32,2,8,512]{3,2,1,0:T(8,128)(2,1)S(1)} %broadcast_in_dim.54), channel_id=1, replica_groups=mesh['row'=32,'col'=8] {'row'}, dimensions={0} | all-to-all | bytes 1048576 | tf_op jit(solution)/shard_map/all_to_all | solution.py:44
  115.9 0.2 all-gather.6.cloned.1.call-start
  116.2 0.7 constant_dynamic-slice_fusion
  117.0 0.2 slice_reduce_fusion.1
  117.2 0.1 add_convert_fusion
  117.3 2.4 copy.25
  119.7 45.7 %all-gather.8.cloned.1.call-done = bf16[256,2,8,512]{3,2,1,0:T(8,128)(2,1)} async-done(((bf16[32,2,8,512]{3,2,1,0:T(8,128)(2,1)}), bf16[256,2,8,512]{3,2,1,0:T(8,128)(2,1)}) %all-gather.8.cloned.1.call-update) | async-done | bytes 4194320 | tf_op jit(solution)/shard_map/all_gather | solution.py:45
  165.4 18.9 %fusion.1 = f32[2,2048,2048]{2,1,0:T(8,128)} fusion(bf16[256,2,8,512]{3,2,1,0:T(8,128)(2,1)} %all-gather.8.cloned.1.call-done), kind=kOutput, calls=%fused_computation.2 | convolution fusion | flops 8589934592 | bytes 37748736 | tf_op jit(solution)/shard_map/spi,sqi->spq/dot_general | solution.py:57
  184.3 17.1 %fusion.5 = bf16[2,2048,288]{1,2,0:T(8,128)(2,1)} fusion(bf16[2,2048,288]{2,1,0:T(8,128)(2,1)S(1)} %bitcast.30, f32[2,2048,2048]{2,1,0:T(8,128)} %fusion.1, f32[2,2048]{1,0:T(2,128)S(1)} %add_convert_fusion), kind=kOutput, calls=%fused_computation.7 | convolution fusion | flops 4900126720 | bytes 38289408 | tf_op jit(solution)/shard_map/spq,sqn->spn/dot_general | solution.py:61
  201.4 3.5 %copy.27 = bf16[2,2048,288]{2,1,0:T(8,128)(2,1)S(1)} copy(bf16[2,2048,288]{1,2,0:T(8,128)(2,1)} %fusion.5) | data formatting | bytes 4718592 | tf_op jit(solution)/shard_map/convert_element_type | solution.py:63
  204.9 2.2 copy.28
  207.1 65.3 %all-gather.6.cloned.1.call-done = bf16[2,2048,1152]{2,1,0:T(8,128)(2,1)} async-done(((bf16[2,64,1152]{2,1,0:T(8,128)(2,1)}), bf16[2,2048,1152]{2,1,0:T(8,128)(2,1)}) %all-gather.6.cloned.1.call-update) | async-done | bytes 9437200 | tf_op jit(solution)/shard_map/all_gather | solution.py:29
  272.4 9.1 %fusion.6 = bf16[1152,2,288]{0,2,1:T(8,128)(2,1)} fusion(bf16[2,2048,288]{2,1,0:T(8,128)(2,1)} %bitcast.31, bf16[2,2048,1152]{2,1,0:T(8,128)(2,1)} %all-gather.6.cloned.1.call-done), kind=kOutput, calls=%fused_computation.8 | convolution fusion | flops 2719236096 | bytes 13123584 | tf_op jit(solution)/shard_map/spm,spn->msn/dot_general | solution.py:70
  (17 shorter events, 0.2 us)
Async XLA Ops:
  6.5 1.7 copy-start
  6.5 110.7 %all-gather.10.cloned.1.call-start = ((), (), s32[]{:S(2)}) async-start(), calls=%async_computation.5 | async-start | bytes 3538944 | tf_op jit(solution)/shard_map/all_gather | solution.py:34
  8.8 36.7 %copy-start.3 = (s32[2]{0:T(128)S(1)}, s32[2]{0:T(128)}, u32[]{:S(2)}) copy-start(s32[2]{0:T(128)} %param.6) | copy-start | bytes 28
  38.9 78.1 %copy-start.2 = (s32[2,2]{1,0:T(2,128)S(1)}, s32[2,2]{1,0:T(2,128)}, u32[]{:S(2)}) copy-start(s32[2,2]{1,0:T(2,128)} %param.7) | copy-start | bytes 52
  39.9 50.5 %all-to-all-start.1 = ((f32[32,2,8,512]{3,2,1,0:T(8,128)}), f32[32,2,8,512]{3,2,1,0:T(8,128)S(1)}, u32[]{:S(2)}, u32[]{:S(2)}) async-start(f32[32,2,8,512]{3,2,1,0:T(8,128)} %copy.23), calls=%async_computation.1 | async-start | bytes 2097152 | tf_op jit(solution)/shard_map/all_to_all | solution.py:39
  45.5 119.8 %all-gather.8.cloned.1.call-start = ((), (), s32[]{:S(2)}) async-start(), calls=%async_computation.4 | async-start | bytes 4718592 | tf_op jit(solution)/shard_map/all_gather | solution.py:45
  115.9 156.5 %all-gather.6.cloned.1.call-start = ((), (), s32[]{:S(2)}) async-start(), calls=%async_computation.3 | async-start | bytes 9732096 | tf_op jit(solution)/shard_map/all_gather | solution.py:29
  272.4 9.1 %copy-start.1 = (bf16[2,64,9216]{2,1,0:T(8,128)(2,1)S(1)}, bf16[2,64,9216]{2,1,0:T(8,128)(2,1)}, u32[]{:S(2)}) copy-start(bf16[2,64,9216]{2,1,0:T(8,128)(2,1)} %param.4) | copy-start | bytes 7077892
Sparse Core Ops, SparseCore 0:
  37.4 50.0 all-gather.9
  116.1 49.2 all-gather.7
  168.2 104.1 all-gather.5

commit v3 on v2

--- a/solution.py
+++ b/solution.py
@@ -26,7 +26,9 @@
     norm_factor = 1.0 / math.sqrt(points)
 
     own_cols = lax.dynamic_slice_in_dim(colloc, col_index * col_width, col_width, 2)
-    basis_cols = lax.all_gather(own_cols, "row", axis=1, tiled=True)
+    basis_cols = []
+    for spin in range(spin_count):
+        basis_cols.append(lax.all_gather(own_cols[spin], "row", axis=0, tiled=True))
 
     own_rows = lax.dynamic_slice_in_dim(colloc, col_index * sub_rows, sub_rows, 1)
     send = own_rows.reshape(spin_count, sub_rows, row_count, row_width).transpose(2, 0, 1, 3)
@@ -36,8 +38,10 @@
     partial_value = jnp.einsum(
         "xspm,smi->xspi", regrouped, coefficients, preferred_element_type=jnp.float32
     )
-    received = lax.all_to_all(partial_value, "row", split_axis=0, concat_axis=0, tiled=True)
-    summed = jnp.sum(received, axis=0)
+    received = lax.all_to_all(
+        partial_value.astype(jnp.bfloat16), "row", split_axis=0, concat_axis=0, tiled=True
+    )
+    summed = jnp.sum(received.astype(jnp.float32), axis=0)
     occupied_mask = jnp.arange(slots, dtype=jnp.int32)[None, :] < occupied[:, None]
     orbitals_own = jnp.where(occupied_mask[:, None, :], summed, 0.0).astype(jnp.bfloat16)
     spread = jnp.broadcast_to(orbitals_own[None], (row_count,) + orbitals_own.shape)
@@ -66,10 +70,14 @@
         .transpose(0, 2, 1, 3, 4)
         .reshape(spin_count, points, -1)
     )
-    return (
-        jnp.einsum("spm,spn->msn", basis_cols, weighted, preferred_element_type=jnp.float32)
-        * norm_factor
-    ).astype(jnp.bfloat16)
+    blocks = [
+        (
+            jnp.einsum("pm,pn->mn", basis_cols[spin], weighted[spin], preferred_element_type=jnp.float32)
+            * norm_factor
+        ).astype(jnp.bfloat16)
+        for spin in range(spin_count)
+    ]
+    return jnp.stack(blocks, axis=1)
 
 
 def solution(mesh):

time: 288 us -> 349 us (1.21)
  waiting for transfers between devices: 156 us -> 216 us
    all_gather x1 -> x2, waiting for transfers between devices: 65.3 us -> 132 us  [local(): basis_cols.append(lax.all_gather(own_cols[spin], 'row', axis=0, tiled=True))]
    all_to_all x1, waiting for transfers between devices: 44.8 us -> 38.6 us  [local(): lax.all_to_all(partial_value.astype(jnp.bfloat16), 'row', split_axis=0, c...]
    slice x0 -> x4, local copies, waits for them, and re-layouts: none -> 3.76 us  [the longest x3 2.04 us: local(): weighted[spin]]
    dot_general x1 -> x2, matrix products: 9.13 us -> 8.71 us  [local(): jnp.einsum('pm,pn->mn', basis_cols[spin], weighted[spin], preferred_eleme...]
  transfers between devices with their start and end apart: 4 -> 5, of which waited for: 3 -> 4; matrix products, arithmetic and copies ran while one was open for 17% -> 15% of each run, Pallas kernels for 0% -> 0%
where the time goes in v3:
time: 349 us
  waiting for transfers between devices  216 us (62%)
  blocking collectives  53.5 us (15%)
  matrix products  46 us (13%)
  between operations  13.3 us (4%)
  local copies, waits for them, and re-layouts  12.5 us (4%)
  starting transfers between devices  5.87 us (2%)
    all_gather x2, waiting for transfers between devices, local(): basis_cols.append(lax.all_gather(own_cols[spin], 'row', axis=0, tiled=True))  132 us
    all_gather x1, waiting for transfers between devices, local(): orbitals_all = lax.all_gather(orbitals_group, 'col', axis=0)  44.7 us
    all_to_all x1, waiting for transfers between devices, local(): lax.all_to_all(partial_value.astype(jnp.bfloat16), 'row', split_axis=0, c...  38.6 us
    all_to_all x1, blocking collectives, local(): lax.all_to_all(send, 'row', split_axis=0, concat_axis=0, tiled=True)  28.2 us
    all_to_all x1, blocking collectives, local(): lax.all_to_all(spread, 'row', split_axis=0, concat_axis=0, tiled=True)  25.3 us
    dot_general x1, matrix products, local(): jnp.einsum('spi,sqi->spq', orbitals_perm, orbitals_perm, preferred_elemen...  18.8 us
    dot_general x1, matrix products, local(): jnp.einsum('spq,sqn->spn', mixed_kernel, basis_perm, preferred_element_ty...  17.1 us
    dot_general x2, matrix products, local(): jnp.einsum('pm,pn->mn', basis_cols[spin], weighted[spin], preferred_eleme...  8.71 us
  transfers between devices with their start and end apart: 5, of which 4 were waited for; matrix products, arithmetic and copies ran while one was open for 15% of the time, Pallas kernels for 0%

profile of v3, /device:TPU:1, one launch (start us, length us, event | category | flops | bytes accessed | tf_op | source)
XLA Modules:
  0.0 349.0 jit_solution(7317219647884602569)
XLA Ops:
  6.5 1.0 constant_dynamic-slice_fusion.1
  7.6 0.6 reshape.250
  8.4 28.2 %all_to_all.15 = bf16[32,2,8,288]{3,2,1,0:T(8,128)(2,1)} all-to-all(bf16[32,2,8,288]{3,2,1,0:T(8,128)(2,1)S(1)} %copy.20), channel_id=1, replica_groups=mesh['row'=32,'col'=8] {'row'}, dimensions={0} | all-to-all | bytes 589824 | tf_op jit(solution)/shard_map/all_to_all | solution.py:35
  36.6 1.4 fusion.27
  38.1 0.9 copy.22
  38.9 5.6 %all-to-all-start.1 = ((bf16[32,2,8,512]{3,2,1,0:T(8,128)(2,1)}), bf16[32,2,8,512]{3,2,1,0:T(8,128)(2,1)S(1)}, u32[]{:S(2)}, u32[]{:S(2)}) async-start(bf16[32,2,8,512]{3,2,1,0:T(8,128)(2,1)} %copy.22), calls=%async_computation.1 | async-start | bytes 1048576 | tf_op jit(solution)/shard_map/all_to_all | solution.py:41
  44.6 38.6 %all-to-all-done.1 = bf16[32,2,8,512]{3,2,1,0:T(8,128)(2,1)S(1)} async-done(((bf16[32,2,8,512]{3,2,1,0:T(8,128)(2,1)}), bf16[32,2,8,512]{3,2,1,0:T(8,128)(2,1)S(1)}, u32[]{:S(2)}, u32[]{:S(2)}) %all-to-all-start.1) | async-done | bytes 524320 | tf_op jit(solution)/shard_map/all_to_all | solution.py:41
  83.4 25.3 %all_to_all.16 = bf16[32,2,8,512]{3,2,1,0:T(8,128)(2,1)} all-to-all(bf16[32,2,8,512]{3,2,1,0:T(8,128)(2,1)S(1)} %broadcast_in_dim.54), channel_id=1, replica_groups=mesh['row'=32,'col'=8] {'row'}, dimensions={0} | all-to-all | bytes 1048576 | tf_op jit(solution)/shard_map/all_to_all | solution.py:48
  108.8 1.7 constant_dynamic-slice_fusion
  110.5 0.2 all-gather.15.cloned.1.call-start
  110.8 0.3 all-gather.15.cloned.1.call-update
  111.5 2.4 copy.24
  113.9 44.7 %all-gather.11.cloned.1.call-done = bf16[256,2,8,512]{3,2,1,0:T(8,128)(2,1)} async-done(((bf16[32,2,8,512]{3,2,1,0:T(8,128)(2,1)}), bf16[256,2,8,512]{3,2,1,0:T(8,128)(2,1)}) %all-gather.11.cloned.1.call-update) | async-done | bytes 4194320 | tf_op jit(solution)/shard_map/all_gather | solution.py:49
  158.6 18.8 %fusion.5 = f32[2,2048,2048]{2,1,0:T(8,128)} fusion(bf16[256,2,8,512]{3,2,1,0:T(8,128)(2,1)} %all-gather.11.cloned.1.call-done), kind=kOutput, calls=%fused_computation.6 | convolution fusion | flops 8589934592 | bytes 37748736 | tf_op jit(solution)/shard_map/spi,sqi->spq/dot_general | solution.py:61
  177.4 17.1 %fusion.8 = bf16[2,2048,288]{1,2,0:T(8,128)(2,1)} fusion(bf16[2,2048,288]{2,1,0:T(8,128)(2,1)S(1)} %bitcast.51, f32[2,2048,2048]{2,1,0:T(8,128)} %fusion.5, f32[2,2048]{1,0:T(2,128)S(1)} %add_convert_fusion), kind=kOutput, calls=%fused_computation.9 | convolution fusion | flops 4900126720 | bytes 38289408 | tf_op jit(solution)/shard_map/spq,sqn->spn/dot_general | solution.py:65
  194.5 3.5 %copy.26 = bf16[2,2048,288]{2,1,0:T(8,128)(2,1)S(1)} copy(bf16[2,2048,288]{1,2,0:T(8,128)(2,1)} %fusion.8) | data formatting | bytes 4718592 | tf_op jit(solution)/shard_map/convert_element_type | solution.py:67
  198.0 0.3 fusion.54
  198.3 1.4 copy.27
  199.8 0.3 copy.28
  200.0 49.2 %all-gather.9.cloned.1.call-done = bf16[1,2048,1152]{2,1,0:T(8,128)(2,1)} async-done(((bf16[1,64,1152]{2,1,0:T(8,128)(2,1)}), bf16[1,2048,1152]{2,1,0:T(8,128)(2,1)}) %all-gather.9.cloned.1.call-update) | async-done | bytes 4718608 | tf_op jit(solution)/shard_map/all_gather | solution.py:31
  249.3 4.6 %fusion.21 = bf16[1152,1,288]{0,2,1:T(8,128)(2,1)S(1)} fusion(bf16[2048,288]{1,0:T(8,128)(2,1)} %bitcast.53, bf16[1,2048,1152]{2,1,0:T(8,128)(2,1)} %all-gather.9.cloned.1.call-done), kind=kOutput, calls=%fused_computation.14 | convolution fusion | flops 1359618048 | bytes 6561792 | tf_op jit(solution)/shard_map/pm,pn->mn/dot_general | solution.py:75
  253.8 83.2 %all-gather.15.cloned.1.call-done = bf16[1,2048,1152]{2,1,0:T(8,128)(2,1)} async-done(((bf16[1,64,1152]{2,1,0:T(8,128)(2,1)}), bf16[1,2048,1152]{2,1,0:T(8,128)(2,1)}) %all-gather.15.cloned.1.call-update) | async-done | bytes 4718608 | tf_op jit(solution)/shard_map/all_gather | solution.py:31
  337.1 4.1 %fusion.24 = bf16[1152,1,288]{0,2,1:T(8,128)(2,1)S(1)} fusion(bf16[2048,288]{1,0:T(8,128)(2,1)S(1)} %bitcast.52, bf16[1,2048,1152]{2,1,0:T(8,128)(2,1)} %all-gather.15.cloned.1.call-done), kind=kOutput, calls=%fused_computation.15 | convolution fusion | flops 1359618048 | bytes 6561792 | tf_op jit(solution)/shard_map/pm,pn->mn/dot_general | solution.py:75
  341.2 1.2 pad_maximum_fusion
  (24 shorter events, 0.8 us)
Async XLA Ops:
  6.5 30.1 %copy-start = (bf16[2,288,512]{2,1,0:T(8,128)(2,1)S(1)}, bf16[2,288,512]{2,1,0:T(8,128)(2,1)}, u32[]{:S(2)}) copy-start(bf16[2,288,512]{2,1,0:T(8,128)(2,1)} %param.5) | copy-start | bytes 1769476
  6.5 104.9 %all-gather.13.cloned.1.call-start = ((), (), s32[]{:S(2)}) async-start(), calls=%async_computation.5 | async-start | bytes 3538944 | tf_op jit(solution)/shard_map/all_gather | solution.py:36
  7.6 36.9 %copy-start.3 = (s32[2]{0:T(128)S(1)}, s32[2]{0:T(128)}, u32[]{:S(2)}) copy-start(s32[2]{0:T(128)} %param.6) | copy-start | bytes 28
  38.0 73.1 %copy-start.2 = (s32[2,2]{1,0:T(2,128)S(1)}, s32[2,2]{1,0:T(2,128)}, u32[]{:S(2)}) copy-start(s32[2,2]{1,0:T(2,128)} %param.7) | copy-start | bytes 52
  38.9 44.3 %all-to-all-start.1 = ((bf16[32,2,8,512]{3,2,1,0:T(8,128)(2,1)}), bf16[32,2,8,512]{3,2,1,0:T(8,128)(2,1)S(1)}, u32[]{:S(2)}, u32[]{:S(2)}) async-start(bf16[32,2,8,512]{3,2,1,0:T(8,128)(2,1)} %copy.22), calls=%async_computation.1 | async-start | bytes 1048576 | tf_op jit(solution)/shard_map/all_to_all | solution.py:41
  44.5 114.1 %all-gather.11.cloned.1.call-start = ((), (), s32[]{:S(2)}) async-start(), calls=%async_computation.4 | async-start | bytes 4718592 | tf_op jit(solution)/shard_map/all_gather | solution.py:49
  108.7 140.5 %all-gather.9.cloned.1.call-start = ((), (), s32[]{:S(2)}) async-start(), calls=%async_computation.3 | async-start | bytes 4866048 | tf_op jit(solution)/shard_map/all_gather | solution.py:31
  110.5 226.6 %all-gather.15.cloned.1.call-start = ((), (), s32[]{:S(2)}) async-start(), calls=%async_computation.6 | async-start | bytes 4866048 | tf_op jit(solution)/shard_map/all_gather | solution.py:31
  337.1 5.3 %copy-start.1 = (bf16[2,288,512]{2,1,0:T(8,128)(2,1)S(1)}, bf16[2,288,512]{2,1,0:T(8,128)(2,1)}, u32[]{:S(2)}) copy-start(bf16[2,288,512]{2,1,0:T(8,128)(2,1)} %param.5) | copy-start | bytes 1769476
Sparse Core Ops, SparseCore 0:
  36.7 44.6 all-gather.12
  108.9 49.6 all-gather.10
  161.4 87.8 all-gather.8
  251.9 85.1 all-gather.14

commit v4 on v1

--- a/solution.py
+++ b/solution.py
@@ -22,32 +22,35 @@
     panel_len = points // 2
     screen_len = panel_len // 8
     col_width = basis // col_count
+    row_width = basis // row_count
     norm_factor = 1.0 / math.sqrt(points)
 
     own_cols = lax.dynamic_slice_in_dim(colloc, col_index * col_width, col_width, 2)
     basis_cols = lax.all_gather(own_cols, "row", axis=1, tiled=True)
 
-    own_rows = lax.dynamic_slice_in_dim(colloc, col_index * sub_rows, sub_rows, 1)
-    regrouped = lax.all_to_all(own_rows, "row", split_axis=2, concat_axis=1, tiled=True)
+    send = colloc.reshape(spin_count, own_points, row_count, row_width).transpose(2, 0, 1, 3)
+    basis_all = lax.all_to_all(send, "row", split_axis=0, concat_axis=0, tiled=True)
+    basis_rows = jnp.moveaxis(basis_all, 1, 0).reshape(spin_count, points, row_width)
+    regrouped = lax.dynamic_slice_in_dim(basis_all, col_index * sub_rows, sub_rows, 2)
+
     partial_value = jnp.einsum(
-        "spm,smi->spi", regrouped, coefficients, preferred_element_type=jnp.float32
+        "xspm,smi->xspi", regrouped, coefficients, preferred_element_type=jnp.float32
     )
-    summed = lax.psum_scatter(partial_value, "row", scatter_dimension=1, tiled=True)
+    received = lax.all_to_all(
+        partial_value.astype(jnp.bfloat16), "row", split_axis=0, concat_axis=0, tiled=True
+    )
+    summed = jnp.sum(received.astype(jnp.float32), axis=0)
     occupied_mask = jnp.arange(slots, dtype=jnp.int32)[None, :] < occupied[:, None]
     orbitals_own = jnp.where(occupied_mask[:, None, :], summed, 0.0).astype(jnp.bfloat16)
-    orbitals_all = lax.all_gather(orbitals_own, ("row", "col"), axis=1, tiled=True)
-
-    basis_group = lax.all_gather(regrouped, "col", axis=1, tiled=True)
-    basis_rows = (
-        basis_group.reshape(spin_count, col_count, row_count, sub_rows, -1)
-        .transpose(0, 2, 1, 3, 4)
-        .reshape(spin_count, points, -1)
-    )
+    spread = jnp.broadcast_to(orbitals_own[None], (row_count,) + orbitals_own.shape)
+    orbitals_group = lax.all_to_all(spread, "row", split_axis=0, concat_axis=0, tiled=True)
+    orbitals_all = lax.all_gather(orbitals_group, "col", axis=0)
+    orbitals_nat = orbitals_all.transpose(2, 1, 0, 3, 4).reshape(spin_count, points, slots)
 
     positions = point_positions(jnp.arange(points, dtype=jnp.int32), offsets, panel_len)
     kernel = 1.0 / (1.0 + jnp.abs(positions[:, :, None] - positions[:, None, :]) / screen_len)
     density = jnp.einsum(
-        "spi,sqi->spq", orbitals_all, orbitals_all, preferred_element_type=jnp.float32
+        "spi,sqi->spq", orbitals_nat, orbitals_nat, preferred_element_type=jnp.float32
     )
     mixed_kernel = (kernel * density / slots).astype(jnp.bfloat16)
     weighted = jnp.einsum(

time: 1030 us -> 328 us (0.32)
  waiting for transfers between devices: 909 us -> 220 us
  local copies, waits for them, and re-layouts: 43.9 us -> 23 us
  starting transfers between devices: 0.31 us -> 19.5 us
    all_gather x2 -> x1, waiting for transfers between devices: 715 us -> 44.6 us  [local(): orbitals_all = lax.all_gather(orbitals_group, 'col', axis=0)]
    reduce_scatter x1 -> x0, waiting for transfers between devices: 105 us -> none  [local(): lax.psum_scatter(partial_value, 'row', scatter_dimension=1, tiled=True)]
    all_to_all x0 -> x2, waiting for transfers between devices: none -> 91.6 us  [the longest x1 73.7 us: local(): lax.all_to_all(send, 'row', split_axis=0, concat_axis=0, tiled=True)]
    unnamed x13 -> x6, local copies, waits for them, and re-layouts: 29.5 us -> 0.01 us
    all_to_all x0 -> x2, starting transfers between devices: none -> 19.2 us  [the longest x1 12.9 us: local(): lax.all_to_all(send, 'row', split_axis=0, concat_axis=0, tiled=True)]
    transpose x0 -> x3, local copies, waits for them, and re-layouts: none -> 13.3 us  [the longest x1 4.75 us: local(): orbitals_all.transpose(2, 1, 0, 3, 4).reshape(spin_count, points, slots)]
  transfers between devices with their start and end apart: 4 -> 4, of which waited for: 3 -> 4; matrix products, arithmetic and copies ran while one was open for 3% -> 9% of each run, Pallas kernels for 0% -> 0%
where the time goes in v4:
time: 328 us
  waiting for transfers between devices  220 us (67%)
  matrix products  28 us (9%)
  blocking collectives  23.6 us (7%)
  local copies, waits for them, and re-layouts  23 us (7%)
  starting transfers between devices  19.5 us (6%)
  between operations  13.5 us (4%)
    all_gather x1, waiting for transfers between devices, local(): basis_cols = lax.all_gather(own_cols, 'row', axis=1, tiled=True)  83.6 us
    all_to_all x1, waiting for transfers between devices, local(): lax.all_to_all(send, 'row', split_axis=0, concat_axis=0, tiled=True)  73.7 us
    all_gather x1, waiting for transfers between devices, local(): orbitals_all = lax.all_gather(orbitals_group, 'col', axis=0)  44.6 us
    all_to_all x1, blocking collectives, local(): lax.all_to_all(spread, 'row', split_axis=0, concat_axis=0, tiled=True)  23.6 us
    dot_general x1, matrix products, local(): jnp.einsum('spq,sqn->spn', mixed_kernel, basis_rows, preferred_element_ty...  18.6 us
    all_to_all x1, waiting for transfers between devices, local(): lax.all_to_all(partial_value.astype(jnp.bfloat16), 'row', split_axis=0, c...  18 us
    all_to_all x1, starting transfers between devices, local(): lax.all_to_all(send, 'row', split_axis=0, concat_axis=0, tiled=True)  12.9 us
    dot_general x1, matrix products, local(): jnp.einsum('spm,spn->msn', basis_cols, weighted, preferred_element_type=j...  7.93 us
  transfers between devices with their start and end apart: 4, of which 4 were waited for; matrix products, arithmetic and copies ran while one was open for 9% of the time, Pallas kernels for 0%

profile of v4, /device:TPU:1, one launch (start us, length us, event | category | flops | bytes accessed | tf_op | source)
XLA Modules:
  0.0 327.8 jit_solution(1096078357906385161)
XLA Ops:
  6.5 6.9 %reshape.192 = bf16[2,64,32,288]{3,2,1,0:T(8,128)(2,1)} reshape(bf16[2,64,9216]{2,1,0:T(8,128)(2,1)} %param.4) | data formatting | bytes 4718592 | tf_op jit(solution)/shard_map/reshape | solution.py:31
  13.5 4.7 %copy.14 = bf16[32,2,64,288]{3,2,1,0:T(8,128)(2,1)} copy(bf16[32,2,64,288]{3,0,2,1:T(8,128)(2,1)} %bitcast.29) | data formatting | bytes 4718592 | tf_op jit(solution)/shard_map/transpose | solution.py:31
  18.1 12.9 %all-to-all-start = ((bf16[32,2,64,288]{3,2,1,0:T(8,128)(2,1)}), bf16[32,2,64,288]{3,2,1,0:T(8,128)(2,1)}, u32[]{:S(2)}, u32[]{:S(2)}) async-start(bf16[32,2,64,288]{3,2,1,0:T(8,128)(2,1)} %copy.14), calls=%async_computation | async-start | bytes 6291456 | tf_op jit(solution)/shard_map/all_to_all | solution.py:32
  31.1 73.7 %all-to-all-done = bf16[32,2,64,288]{3,2,1,0:T(8,128)(2,1)} async-done(((bf16[32,2,64,288]{3,2,1,0:T(8,128)(2,1)}), bf16[32,2,64,288]{3,2,1,0:T(8,128)(2,1)}, u32[]{:S(2)}, u32[]{:S(2)}) %all-to-all-start) | async-done | bytes 2359328 | tf_op jit(solution)/shard_map/all_to_all | solution.py:32
  104.7 1.4 fusion.4
  106.2 0.9 copy.16
  107.0 6.3 %all-to-all-start.1 = ((bf16[32,2,8,512]{3,2,1,0:T(8,128)(2,1)}), bf16[32,2,8,512]{3,2,1,0:T(8,128)(2,1)S(1)}, u32[]{:S(2)}, u32[]{:S(2)}) async-start(bf16[32,2,8,512]{3,2,1,0:T(8,128)(2,1)} %copy.16), calls=%async_computation.1 | async-start | bytes 1048576 | tf_op jit(solution)/shard_map/all_to_all | solution.py:39
  113.4 0.0 all-gather.6.cloned.1.call-start
  113.4 0.1 iota_compare_fusion
  113.5 18.0 %all-to-all-done.1 = bf16[32,2,8,512]{3,2,1,0:T(8,128)(2,1)S(1)} async-done(((bf16[32,2,8,512]{3,2,1,0:T(8,128)(2,1)}), bf16[32,2,8,512]{3,2,1,0:T(8,128)(2,1)S(1)}, u32[]{:S(2)}, u32[]{:S(2)}) %all-to-all-start.1) | async-done | bytes 524320 | tf_op jit(solution)/shard_map/all_to_all | solution.py:39
  131.4 0.1 convert_reduce_fusion
  131.5 0.1 broadcast_in_dim.54
  131.6 23.6 %all_to_all.15 = bf16[32,2,8,512]{3,2,1,0:T(8,128)(2,1)} all-to-all(bf16[32,2,8,512]{3,2,1,0:T(8,128)(2,1)S(1)} %broadcast_in_dim.54), channel_id=1, replica_groups=mesh['row'=32,'col'=8] {'row'}, dimensions={0} | all-to-all | bytes 1048576 | tf_op jit(solution)/shard_map/all_to_all | solution.py:46
  155.2 0.0 all-gather.6.cloned.1.call-update
  155.2 0.2 all-gather.4.cloned.1.call-start
  155.5 1.7 constant_dynamic-slice_fusion
  157.2 0.2 slice_reduce_fusion.1
  157.4 0.1 add_convert_fusion
  157.5 3.9 %copy.18 = bf16[2,32,64,288]{3,2,1,0:T(8,128)(2,1)} copy(bf16[2,32,64,288]{3,2,0,1:T(8,128)(2,1)} %bitcast.7) | data formatting | bytes 4718592 | tf_op jit(solution)/shard_map/transpose | solution.py:33
  161.4 44.6 %all-gather.6.cloned.1.call-done = bf16[256,2,8,512]{3,2,1,0:T(8,128)(2,1)} async-done(((bf16[32,2,8,512]{3,2,1,0:T(8,128)(2,1)}), bf16[256,2,8,512]{3,2,1,0:T(8,128)(2,1)}) %all-gather.6.cloned.1.call-update) | async-done | bytes 4194320 | tf_op jit(solution)/shard_map/all_gather | solution.py:47
  206.0 4.8 %copy.17 = bf16[2,32,8,8,512]{4,3,2,1,0:T(8,128)(2,1)} copy(bf16[2,32,8,8,512]{4,3,0,1,2:T(8,128)(2,1)} %bitcast.30) | data formatting | bytes 8388608 | tf_op jit(solution)/shard_map/transpose | solution.py:48
  210.8 18.6 %fusion.1 = bf16[2,2048,288]{1,2,0:T(8,128)(2,1)S(1)} fusion(bf16[2,2048,288]{2,1,0:T(8,128)(2,1)} %bitcast.32, f32[2,2048]{1,0:T(2,128)S(1)} %add_convert_fusion, bf16[2,2048,512]{2,1,0:T(8,128)(2,1)} %bitcast.31), kind=kOutput, calls=%fused_computation.3 | convolution fusion | flops 13490061312 | bytes 8929280 | tf_op jit(solution)/shard_map/spq,sqn->spn/dot_general | solution.py:56
  229.4 83.6 %all-gather.4.cloned.1.call-done = bf16[2,2048,1152]{2,1,0:T(8,128)(2,1)} async-done(((bf16[2,64,1152]{2,1,0:T(8,128)(2,1)}), bf16[2,2048,1152]{2,1,0:T(8,128)(2,1)}) %all-gather.4.cloned.1.call-update) | async-done | bytes 9437200 | tf_op jit(solution)/shard_map/all_gather | solution.py:29
  313.1 7.9 %fusion.3 = bf16[1152,2,288]{0,2,1:T(8,128)(2,1)} fusion(bf16[2,2048,288]{1,2,0:T(8,128)(2,1)S(1)} %fusion.1, bf16[2,2048,1152]{2,1,0:T(8,128)(2,1)} %all-gather.4.cloned.1.call-done), kind=kOutput, calls=%fused_computation.5 | convolution fusion | flops 2719236096 | bytes 13123584 | tf_op jit(solution)/shard_map/spm,spn->msn/dot_general | solution.py:60
  (10 shorter events, 0.1 us)
Async XLA Ops:
  6.5 98.2 %copy-start = (bf16[2,288,512]{2,1,0:T(8,128)(2,1)S(1)}, bf16[2,288,512]{2,1,0:T(8,128)(2,1)}, u32[]{:S(2)}) copy-start(bf16[2,288,512]{2,1,0:T(8,128)(2,1)} %param.5) | copy-start | bytes 1769476
  18.1 95.3 %copy-start.2 = (s32[2]{0:T(128)S(1)}, s32[2]{0:T(128)}, u32[]{:S(2)}) copy-start(s32[2]{0:T(128)} %param.6) | copy-start | bytes 28
  18.1 86.6 %all-to-all-start = ((bf16[32,2,64,288]{3,2,1,0:T(8,128)(2,1)}), bf16[32,2,64,288]{3,2,1,0:T(8,128)(2,1)}, u32[]{:S(2)}, u32[]{:S(2)}) async-start(bf16[32,2,64,288]{3,2,1,0:T(8,128)(2,1)} %copy.14), calls=%async_computation | async-start | bytes 6291456 | tf_op jit(solution)/shard_map/all_to_all | solution.py:32
  31.1 126.1 %copy-start.1 = (s32[2,2]{1,0:T(2,128)S(1)}, s32[2,2]{1,0:T(2,128)}, u32[]{:S(2)}) copy-start(s32[2,2]{1,0:T(2,128)} %param.7) | copy-start | bytes 52
  107.0 24.4 %all-to-all-start.1 = ((bf16[32,2,8,512]{3,2,1,0:T(8,128)(2,1)}), bf16[32,2,8,512]{3,2,1,0:T(8,128)(2,1)S(1)}, u32[]{:S(2)}, u32[]{:S(2)}) async-start(bf16[32,2,8,512]{3,2,1,0:T(8,128)(2,1)} %copy.16), calls=%async_computation.1 | async-start | bytes 1048576 | tf_op jit(solution)/shard_map/all_to_all | solution.py:39
  113.4 92.7 %all-gather.6.cloned.1.call-start = ((), (), s32[]{:S(2)}) async-start(), calls=%async_computation.4 | async-start | bytes 4718592 | tf_op jit(solution)/shard_map/all_gather | solution.py:47
  155.2 157.8 %all-gather.4.cloned.1.call-start = ((), (), s32[]{:S(2)}) async-start(), calls=%async_computation.3 | async-start | bytes 9732096 | tf_op jit(solution)/shard_map/all_gather | solution.py:29
Sparse Core Ops, SparseCore 0:
  155.4 50.6 all-gather.5
  208.8 104.1 all-gather.3

commit v5 on v4

--- a/solution.py
+++ b/solution.py
@@ -9,6 +9,12 @@
 def point_positions(point_ids, offsets, panel_len):
     first = jnp.where(point_ids[None, :] // panel_len == 0, offsets[:, 0:1], offsets[:, 1:2])
     return (first + point_ids[None, :] % panel_len).astype(jnp.float32)
+
+
+def gather_col(x, col_index, col_count):
+    slot = jnp.arange(col_count, dtype=jnp.int32).reshape((col_count,) + (1,) * x.ndim)
+    padded = jnp.where(slot == col_index, x[None], jnp.zeros_like(x)[None])
+    return lax.psum(padded, "col")
 
 
 def local(colloc, coefficients, occupied, offsets):
@@ -28,10 +34,11 @@
     own_cols = lax.dynamic_slice_in_dim(colloc, col_index * col_width, col_width, 2)
     basis_cols = lax.all_gather(own_cols, "row", axis=1, tiled=True)
 
-    send = colloc.reshape(spin_count, own_points, row_count, row_width).transpose(2, 0, 1, 3)
-    basis_all = lax.all_to_all(send, "row", split_axis=0, concat_axis=0, tiled=True)
-    basis_rows = jnp.moveaxis(basis_all, 1, 0).reshape(spin_count, points, row_width)
-    regrouped = lax.dynamic_slice_in_dim(basis_all, col_index * sub_rows, sub_rows, 2)
+    own_rows = lax.dynamic_slice_in_dim(colloc, col_index * sub_rows, sub_rows, 1)
+    send = own_rows.reshape(spin_count, sub_rows, row_count, row_width).transpose(2, 0, 1, 3)
+    regrouped = lax.all_to_all(send, "row", split_axis=0, concat_axis=0, tiled=True)
+    basis_all = gather_col(regrouped, col_index, col_count)
+    basis_rows = basis_all.transpose(2, 1, 0, 3, 4).reshape(spin_count, points, row_width)
 
     partial_value = jnp.einsum(
         "xspm,smi->xspi", regrouped, coefficients, preferred_element_type=jnp.float32
@@ -44,7 +51,7 @@
     orbitals_own = jnp.where(occupied_mask[:, None, :], summed, 0.0).astype(jnp.bfloat16)
     spread = jnp.broadcast_to(orbitals_own[None], (row_count,) + orbitals_own.shape)
     orbitals_group = lax.all_to_all(spread, "row", split_axis=0, concat_axis=0, tiled=True)
-    orbitals_all = lax.all_gather(orbitals_group, "col", axis=0)
+    orbitals_all = gather_col(orbitals_group, col_index, col_count)
     orbitals_nat = orbitals_all.transpose(2, 1, 0, 3, 4).reshape(spin_count, points, slots)
 
     positions = point_positions(jnp.arange(points, dtype=jnp.int32), offsets, panel_len)

time: 328 us -> 311 us (0.948)
  waiting for transfers between devices: 220 us -> 195 us
  matrix products: 28 us -> 45.9 us
  local copies, waits for them, and re-layouts: 23 us -> 9.58 us
  starting transfers between devices: 19.5 us -> 11.4 us
  other arithmetic: 0.25 us -> 5.75 us
  blocking collectives: 23.6 us -> 28.1 us
    psum x0 -> x1, waiting for transfers between devices: none -> 149 us  [gather_col(): return lax.psum(padded, 'col')]
    all_gather x1, waiting for transfers between devices: 83.6 us -> 16.6 us  [local(): basis_cols = lax.all_gather(own_cols, 'row', axis=1, tiled=True)]
    all_to_all x1, waiting for transfers between devices: 73.7 us -> 11.1 us  [local(): lax.all_to_all(spread, 'row', split_axis=0, concat_axis=0, tiled=True)]
    all_gather x1 -> x0, waiting for transfers between devices: 44.6 us -> none  [local(): orbitals_all = lax.all_gather(orbitals_group, 'col', axis=0)]
    dot_general x0 -> x1, matrix products: none -> 18.1 us  [local(): jnp.einsum('spi,sqi->spq', orbitals_nat, orbitals_nat, preferred_element_...]
    transpose x3 -> x1, local copies, waits for them, and re-layouts: 13.3 us -> 0.13 us  [local(): own_rows.reshape(spin_count, sub_rows, row_count, row_width)]
    all_to_all x1, starting transfers between devices: 12.9 us -> 5.6 us  [local(): lax.all_to_all(spread, 'row', split_axis=0, concat_axis=0, tiled=True)]
    select_n x0 -> x2, other arithmetic: none -> 5.49 us  [gather_col(): padded = jnp.where(slot == col_index, x[None], jnp.zeros_like(x)[None])]
  transfers between devices with their start and end apart: 4 -> 4, of which waited for: 4 -> 4; matrix products, arithmetic and copies ran while one was open for 9% -> 14% of each run, Pallas kernels for 0% -> 0%
where the time goes in v5:
time: 311 us
  waiting for transfers between devices  195 us (63%)
  matrix products  45.9 us (15%)
  blocking collectives  28.1 us (9%)
  between operations  14.9 us (5%)
  starting transfers between devices  11.4 us (4%)
  local copies, waits for them, and re-layouts  9.58 us (3%)
  other arithmetic  5.75 us (2%)
    psum x1, waiting for transfers between devices, gather_col(): return lax.psum(padded, 'col')  149 us
    all_to_all x1, blocking collectives, local(): lax.all_to_all(send, 'row', split_axis=0, concat_axis=0, tiled=True)  28.1 us
    dot_general x1, matrix products, local(): jnp.einsum('spi,sqi->spq', orbitals_nat, orbitals_nat, preferred_element_...  18.1 us
    all_to_all x1, waiting for transfers between devices, local(): lax.all_to_all(partial_value.astype(jnp.bfloat16), 'row', split_axis=0, c...  18.1 us
    dot_general x1, matrix products, local(): jnp.einsum('spq,sqn->spn', mixed_kernel, basis_rows, preferred_element_ty...  17.5 us
    all_gather x1, waiting for transfers between devices, local(): basis_cols = lax.all_gather(own_cols, 'row', axis=1, tiled=True)  16.6 us
    all_to_all x1, waiting for transfers between devices, local(): lax.all_to_all(spread, 'row', split_axis=0, concat_axis=0, tiled=True)  11.1 us
    dot_general x1, matrix products, local(): jnp.einsum('spm,spn->msn', basis_cols, weighted, preferred_element_type=j...  8.81 us
  transfers between devices with their start and end apart: 4, of which 4 were waited for; matrix products, arithmetic and copies ran while one was open for 14% of the time, Pallas kernels for 0%

profile of v5, /device:TPU:1, one launch (start us, length us, event | category | flops | bytes accessed | tf_op | source)
XLA Modules:
  0.0 310.9 jit_solution(14323157586605716685)
XLA Ops:
  7.4 1.7 copy-done
  9.1 0.6 reshape.201
  9.7 0.1 copy.7
  9.8 28.1 %all_to_all.15 = bf16[32,2,8,288]{3,2,1,0:T(8,128)(2,1)S(1)} all-to-all(bf16[32,2,8,288]{3,2,1,0:T(8,128)(2,1)S(1)} %copy.7), channel_id=1, replica_groups=mesh['row'=32,'col'=8] {'row'}, dimensions={0} | all-to-all | bytes 589824 | tf_op jit(solution)/shard_map/all_to_all | solution.py:39
  37.9 1.5 fusion.4
  39.4 0.9 copy.9
  40.3 5.6 %all-to-all-start.1 = ((bf16[32,2,8,512]{3,2,1,0:T(8,128)(2,1)}), bf16[32,2,8,512]{3,2,1,0:T(8,128)(2,1)S(1)}, u32[]{:S(2)}, u32[]{:S(2)}) async-start(bf16[32,2,8,512]{3,2,1,0:T(8,128)(2,1)} %copy.9), calls=%async_computation.1 | async-start | bytes 1048576 | tf_op jit(solution)/shard_map/all_to_all | solution.py:46
  45.9 18.1 %all-to-all-done.1 = bf16[32,2,8,512]{3,2,1,0:T(8,128)(2,1)S(1)} async-done(((bf16[32,2,8,512]{3,2,1,0:T(8,128)(2,1)}), bf16[32,2,8,512]{3,2,1,0:T(8,128)(2,1)S(1)}, u32[]{:S(2)}, u32[]{:S(2)}) %all-to-all-start.1) | async-done | bytes 524320 | tf_op jit(solution)/shard_map/all_to_all | solution.py:46
  64.1 0.1 convert_reduce_fusion
  64.2 0.9 broadcast_in_dim.105
  65.0 5.6 %all-to-all-start.2 = ((bf16[32,2,8,512]{3,2,1,0:T(8,128)(2,1)}), bf16[32,2,8,512]{3,2,1,0:T(8,128)(2,1)S(1)}, u32[]{:S(2)}, u32[]{:S(2)}) async-start(bf16[32,2,8,512]{3,2,1,0:T(8,128)(2,1)} %broadcast_in_dim.105), calls=%async_computation.2 | async-start | bytes 1048576 | tf_op jit(solution)/shard_map/all_to_all | solution.py:53
  70.7 2.6 broadcast_select_fusion.1
  73.2 4.5 %copy.12 = bf16[2,2048,288]{1,2,0:T(8,128)(2,1)} copy(bf16[2,2048,288]{2,1,0:T(8,128)(2,1)} %bitcast.22) | data formatting | bytes 4718592 | tf_op jit(solution)/shard_map/reshape | solution.py:41
  77.8 11.1 %all-to-all-done.2 = bf16[32,2,8,512]{3,2,1,0:T(8,128)(2,1)S(1)} async-done(((bf16[32,2,8,512]{3,2,1,0:T(8,128)(2,1)}), bf16[32,2,8,512]{3,2,1,0:T(8,128)(2,1)S(1)}, u32[]{:S(2)}, u32[]{:S(2)}) %all-to-all-start.2) | async-done | bytes 524320 | tf_op jit(solution)/shard_map/all_to_all | solution.py:53
  88.8 2.9 broadcast_select_fusion
  91.8 0.2 all-gather.2.cloned.1.call-start
  92.1 0.7 constant_dynamic-slice_fusion
  92.8 0.2 slice_reduce_fusion.1
  93.0 0.1 add_convert_fusion
  93.1 149.3 %all-reduce.3.cloned.1.call-done = (bf16[2,2048,288]{1,2,0:T(8,128)(2,1)}, bf16[2,2048,512]{2,1,0:T(8,128)(2,1)}) async-done(((bf16[2,2048,288]{1,2,0:T(8,128)(2,1)}, bf16[2,2048,512]{2,1,0:T(8,128)(2,1)}), (bf16[2,2048,288]{1,2,0:T(8,128)(2,1)}, bf16[2,2048,512]{2,1,0:T(8,128)(2,1)})) %all-reduce.3.cloned.1.call-update) | async-done | bytes 6553616 | tf_op jit(solution)/shard_map/psum | solution.py:17
  242.4 18.1 %fusion.18 = f32[2,2048,2048]{2,1,0:T(8,128)} fusion(bf16[2,2048,512]{2,1,0:T(8,128)(2,1)} %get-tuple-element.8), kind=kOutput, calls=%fused_computation.36 | convolution fusion | flops 8589934592 | bytes 37748736 | tf_op jit(solution)/shard_map/spi,sqi->spq/dot_general | solution.py:59
  260.6 17.5 %fusion.1 = bf16[2,2048,288]{1,2,0:T(8,128)(2,1)} fusion(bf16[2,2048,288]{1,2,0:T(8,128)(2,1)} %get-tuple-element.7, f32[2,2048,2048]{2,1,0:T(8,128)} %fusion.18, f32[2,2048]{1,0:T(2,128)S(1)} %add_convert_fusion), kind=kOutput, calls=%fused_computation.5 | convolution fusion | flops 4900126720 | bytes 38289408 | tf_op jit(solution)/shard_map/spq,sqn->spn/dot_general | solution.py:63
  278.0 16.6 %all-gather.2.cloned.1.call-done = bf16[2,2048,1152]{2,1,0:T(8,128)(2,1)} async-done(((bf16[2,64,1152]{2,1,0:T(8,128)(2,1)}), bf16[2,2048,1152]{2,1,0:T(8,128)(2,1)}) %all-gather.2.cloned.1.call-update) | async-done | bytes 9437200 | tf_op jit(solution)/shard_map/all_gather | solution.py:35
  294.6 8.8 %fusion.3 = bf16[1152,2,288]{0,2,1:T(8,128)(2,1)} fusion(bf16[2,2048,288]{1,2,0:T(8,128)(2,1)} %fusion.1, bf16[2,2048,1152]{2,1,0:T(8,128)(2,1)} %all-gather.2.cloned.1.call-done), kind=kOutput, calls=%fused_computation.7 | convolution fusion | flops 2719236096 | bytes 13123584 | tf_op jit(solution)/shard_map/spm,spn->msn/dot_general | solution.py:67
  (16 shorter events, 0.2 us)
Async XLA Ops:
  7.4 1.7 copy-start
  7.4 38.5 %copy-start.3 = (s32[2]{0:T(128)S(1)}, s32[2]{0:T(128)}, u32[]{:S(2)}) copy-start(s32[2]{0:T(128)} %param.6) | copy-start | bytes 28
  40.3 23.8 %all-to-all-start.1 = ((bf16[32,2,8,512]{3,2,1,0:T(8,128)(2,1)}), bf16[32,2,8,512]{3,2,1,0:T(8,128)(2,1)S(1)}, u32[]{:S(2)}, u32[]{:S(2)}) async-start(bf16[32,2,8,512]{3,2,1,0:T(8,128)(2,1)} %copy.9), calls=%async_computation.1 | async-start | bytes 1048576 | tf_op jit(solution)/shard_map/all_to_all | solution.py:46
  65.0 23.8 %all-to-all-start.2 = ((bf16[32,2,8,512]{3,2,1,0:T(8,128)(2,1)}), bf16[32,2,8,512]{3,2,1,0:T(8,128)(2,1)S(1)}, u32[]{:S(2)}, u32[]{:S(2)}) async-start(bf16[32,2,8,512]{3,2,1,0:T(8,128)(2,1)} %broadcast_in_dim.105), calls=%async_computation.2 | async-start | bytes 1048576 | tf_op jit(solution)/shard_map/all_to_all | solution.py:53
  70.6 171.8 %all-reduce.3.cloned.1.call-start = ((), (), s32[]{:S(2)}) async-start(), calls=%async_computation.4 | async-start | bytes 13107200 | tf_op jit(solution)/shard_map/psum | solution.py:17
  91.8 1.0 copy-start.2
  91.8 202.8 %all-gather.2.cloned.1.call-start = ((), (), s32[]{:S(2)}) async-start(), calls=%async_computation.3 | async-start | bytes 9732096 | tf_op jit(solution)/shard_map/all_gather | solution.py:35
  294.6 8.8 %copy-start.1 = (bf16[2,64,9216]{2,1,0:T(8,128)(2,1)S(1)}, bf16[2,64,9216]{2,1,0:T(8,128)(2,1)}, u32[]{:S(2)}) copy-start(bf16[2,64,9216]{2,1,0:T(8,128)(2,1)} %param.4) | copy-start | bytes 7077892
Sparse Core Ops, SparseCore 0:
  91.9 150.4 all-reduce.2
Sparse Core Ops, SparseCore 1:
  95.1 199.4 all-gather.1

commit v6 on v4

--- a/solution.py
+++ b/solution.py
@@ -28,10 +28,9 @@
     own_cols = lax.dynamic_slice_in_dim(colloc, col_index * col_width, col_width, 2)
     basis_cols = lax.all_gather(own_cols, "row", axis=1, tiled=True)
 
-    send = colloc.reshape(spin_count, own_points, row_count, row_width).transpose(2, 0, 1, 3)
-    basis_all = lax.all_to_all(send, "row", split_axis=0, concat_axis=0, tiled=True)
-    basis_rows = jnp.moveaxis(basis_all, 1, 0).reshape(spin_count, points, row_width)
-    regrouped = lax.dynamic_slice_in_dim(basis_all, col_index * sub_rows, sub_rows, 2)
+    own_rows = lax.dynamic_slice_in_dim(colloc, col_index * sub_rows, sub_rows, 1)
+    send = own_rows.reshape(spin_count, sub_rows, row_count, row_width).transpose(2, 0, 1, 3)
+    regrouped = lax.all_to_all(send, "row", split_axis=0, concat_axis=0, tiled=True)
 
     partial_value = jnp.einsum(
         "xspm,smi->xspi", regrouped, coefficients, preferred_element_type=jnp.float32
@@ -46,6 +45,10 @@
     orbitals_group = lax.all_to_all(spread, "row", split_axis=0, concat_axis=0, tiled=True)
     orbitals_all = lax.all_gather(orbitals_group, "col", axis=0)
     orbitals_nat = orbitals_all.transpose(2, 1, 0, 3, 4).reshape(spin_count, points, slots)
+
+    every = colloc.reshape(spin_count, own_points, row_count, row_width).transpose(2, 0, 1, 3)
+    basis_all = lax.all_to_all(every, "row", split_axis=0, concat_axis=0, tiled=True)
+    basis_rows = jnp.moveaxis(basis_all, 1, 0).reshape(spin_count, points, row_width)
 
     positions = point_positions(jnp.arange(points, dtype=jnp.int32), offsets, panel_len)
     kernel = 1.0 / (1.0 + jnp.abs(positions[:, :, None] - positions[:, None, :]) / screen_len)

time: 328 us -> 284 us (0.87)
  waiting for transfers between devices: 220 us -> 154 us
  blocking collectives: 23.6 us -> 51.7 us
  starting transfers between devices: 19.5 us -> 12.1 us
    all_gather x1, waiting for transfers between devices: 44.6 us -> 0.01 us  [local(): orbitals_all = lax.all_gather(orbitals_group, 'col', axis=0)]
    all_to_all x0 -> x1, blocking collectives: none -> 28.1 us  [local(): lax.all_to_all(send, 'row', split_axis=0, concat_axis=0, tiled=True)]
    all_gather x1, waiting for transfers between devices: 83.6 us -> 63.4 us  [local(): basis_cols = lax.all_gather(own_cols, 'row', axis=1, tiled=True)]
    all_to_all x1, starting transfers between devices: 12.9 us -> 6.45 us  [local(): lax.all_to_all(every, 'row', split_axis=0, concat_axis=0, tiled=True)]
  transfers between devices with their start and end apart: 4 -> 4, of which waited for: 4 -> 3; matrix products, arithmetic and copies ran while one was open for 9% -> 14% of each run, Pallas kernels for 0% -> 0%
where the time goes in v6:
time: 284 us; the launch traced here: 283 us
  waiting for transfers between devices  154 us (54%)
  blocking collectives  51.7 us (18%)
  matrix products  26.9 us (9%)
  local copies, waits for them, and re-layouts  24.7 us (9%)
  between operations  13.5 us (5%)
  starting transfers between devices  12.1 us (4%)
    all_to_all x1, waiting for transfers between devices, local(): lax.all_to_all(every, 'row', split_axis=0, concat_axis=0, tiled=True)  72.5 us
    all_gather x1, waiting for transfers between devices, local(): basis_cols = lax.all_gather(own_cols, 'row', axis=1, tiled=True)  63.4 us
    all_to_all x1, blocking collectives, local(): lax.all_to_all(send, 'row', split_axis=0, concat_axis=0, tiled=True)  28.1 us
    all_to_all x1, blocking collectives, local(): lax.all_to_all(spread, 'row', split_axis=0, concat_axis=0, tiled=True)  23.6 us
    dot_general x1, matrix products, local(): jnp.einsum('spq,sqn->spn', mixed_kernel, basis_rows, preferred_element_ty...  18.6 us
    all_to_all x1, waiting for transfers between devices, local(): lax.all_to_all(partial_value.astype(jnp.bfloat16), 'row', split_axis=0, c...  18.1 us
    dot_general x1, matrix products, local(): jnp.einsum('spm,spn->msn', basis_cols, weighted, preferred_element_type=j...  7.94 us
    all_to_all x1, starting transfers between devices, local(): lax.all_to_all(every, 'row', split_axis=0, concat_axis=0, tiled=True)  6.45 us
  transfers between devices with their start and end apart: 4, of which 3 were waited for; matrix products, arithmetic and copies ran while one was open for 14% of the time, Pallas kernels for 0%

profile of v6, /device:TPU:1, one launch (start us, length us, event | category | flops | bytes accessed | tf_op | source)
XLA Modules:
  0.0 283.2 jit_solution(13924377578242015513)
XLA Ops:
  6.5 1.8 constant_dynamic-slice_fusion.1
  8.3 1.7 reshape.195
  10.0 0.1 copy.17
  10.2 28.1 %all_to_all.20 = bf16[32,2,8,288]{3,2,1,0:T(8,128)(2,1)S(1)} all-to-all(bf16[32,2,8,288]{3,2,1,0:T(8,128)(2,1)S(1)} %copy.17), channel_id=1, replica_groups=mesh['row'=32,'col'=8] {'row'}, dimensions={0} | all-to-all | bytes 589824 | tf_op jit(solution)/shard_map/all_to_all | solution.py:33
  38.3 0.4 fusion.4
  38.7 0.9 copy.19
  39.6 5.6 %all-to-all-start.1 = ((bf16[32,2,8,512]{3,2,1,0:T(8,128)(2,1)}), bf16[32,2,8,512]{3,2,1,0:T(8,128)(2,1)S(1)}, u32[]{:S(2)}, u32[]{:S(2)}) async-start(bf16[32,2,8,512]{3,2,1,0:T(8,128)(2,1)} %copy.19), calls=%async_computation.1 | async-start | bytes 1048576 | tf_op jit(solution)/shard_map/all_to_all | solution.py:38
  45.2 0.1 iota_compare_fusion
  45.3 18.1 %all-to-all-done.1 = bf16[32,2,8,512]{3,2,1,0:T(8,128)(2,1)S(1)} async-done(((bf16[32,2,8,512]{3,2,1,0:T(8,128)(2,1)}), bf16[32,2,8,512]{3,2,1,0:T(8,128)(2,1)S(1)}, u32[]{:S(2)}, u32[]{:S(2)}) %all-to-all-start.1) | async-done | bytes 524320 | tf_op jit(solution)/shard_map/all_to_all | solution.py:38
  63.4 0.1 convert_reduce_fusion
  63.5 0.1 broadcast_in_dim.54
  63.5 23.6 %all_to_all.21 = bf16[32,2,8,512]{3,2,1,0:T(8,128)(2,1)} all-to-all(bf16[32,2,8,512]{3,2,1,0:T(8,128)(2,1)S(1)} %broadcast_in_dim.54), channel_id=1, replica_groups=mesh['row'=32,'col'=8] {'row'}, dimensions={0} | all-to-all | bytes 1048576 | tf_op jit(solution)/shard_map/all_to_all | solution.py:45
  87.2 0.7 constant_dynamic-slice_fusion
  88.0 5.8 %reshape.197 = bf16[2,64,32,288]{3,2,1,0:T(8,128)(2,1)} reshape(bf16[2,64,9216]{2,1,0:T(8,128)(2,1)S(1)} %copy-done.1) | data formatting | bytes 4718592 | tf_op jit(solution)/shard_map/reshape | solution.py:49
  93.7 4.8 %copy.21 = bf16[32,2,64,288]{3,2,1,0:T(8,128)(2,1)} copy(bf16[32,2,64,288]{3,0,2,1:T(8,128)(2,1)} %bitcast.30) | data formatting | bytes 4718592 | tf_op jit(solution)/shard_map/transpose | solution.py:49
  98.6 6.5 %all-to-all-start.3 = ((bf16[32,2,64,288]{3,2,1,0:T(8,128)(2,1)}), bf16[32,2,64,288]{3,2,1,0:T(8,128)(2,1)}, u32[]{:S(2)}, u32[]{:S(2)}) async-start(bf16[32,2,64,288]{3,2,1,0:T(8,128)(2,1)} %copy.21), calls=%async_computation.3 | async-start | bytes 6291456 | tf_op jit(solution)/shard_map/all_to_all | solution.py:50
  105.0 0.2 slice_reduce_fusion.1
  105.2 0.1 add_convert_fusion
  105.3 72.5 %all-to-all-done.3 = bf16[32,2,64,288]{3,2,1,0:T(8,128)(2,1)} async-done(((bf16[32,2,64,288]{3,2,1,0:T(8,128)(2,1)}), bf16[32,2,64,288]{3,2,1,0:T(8,128)(2,1)}, u32[]{:S(2)}, u32[]{:S(2)}) %all-to-all-start.3) | async-done | bytes 2359328 | tf_op jit(solution)/shard_map/all_to_all | solution.py:50
  177.8 3.9 %copy.22 = bf16[2,32,64,288]{3,2,1,0:T(8,128)(2,1)} copy(bf16[2,32,64,288]{3,2,0,1:T(8,128)(2,1)} %bitcast.8) | data formatting | bytes 4718592 | tf_op jit(solution)/shard_map/transpose | solution.py:51
  181.7 4.8 %copy.20 = bf16[2,32,8,8,512]{4,3,2,1,0:T(8,128)(2,1)} copy(bf16[2,32,8,8,512]{4,3,0,1,2:T(8,128)(2,1)} %bitcast.31) | data formatting | bytes 8388608 | tf_op jit(solution)/shard_map/transpose | solution.py:47
  186.5 18.6 %fusion.1 = bf16[2,2048,288]{1,2,0:T(8,128)(2,1)S(1)} fusion(bf16[2,2048,288]{2,1,0:T(8,128)(2,1)} %bitcast.33, f32[2,2048]{1,0:T(2,128)S(1)} %add_convert_fusion, bf16[2,2048,512]{2,1,0:T(8,128)(2,1)} %bitcast.32), kind=kOutput, calls=%fused_computation.3 | convolution fusion | flops 13490061312 | bytes 8929280 | tf_op jit(solution)/shard_map/spq,sqn->spn/dot_general | solution.py:59
  205.1 63.4 %all-gather.4.cloned.1.call-done = bf16[2,2048,1152]{2,1,0:T(8,128)(2,1)} async-done(((bf16[2,64,1152]{2,1,0:T(8,128)(2,1)}), bf16[2,2048,1152]{2,1,0:T(8,128)(2,1)}) %all-gather.4.cloned.1.call-update) | async-done | bytes 9437200 | tf_op jit(solution)/shard_map/all_gather | solution.py:29
  268.4 7.9 %fusion.3 = bf16[1152,2,288]{0,2,1:T(8,128)(2,1)} fusion(bf16[2,2048,288]{1,2,0:T(8,128)(2,1)S(1)} %fusion.1, bf16[2,2048,1152]{2,1,0:T(8,128)(2,1)} %all-gather.4.cloned.1.call-done), kind=kOutput, calls=%fused_computation.5 | convolution fusion | flops 2719236096 | bytes 13123584 | tf_op jit(solution)/shard_map/spm,spn->msn/dot_general | solution.py:63
  (16 shorter events, 0.2 us)
Async XLA Ops:
  6.5 31.7 %copy-start = (bf16[2,288,512]{2,1,0:T(8,128)(2,1)S(1)}, bf16[2,288,512]{2,1,0:T(8,128)(2,1)}, u32[]{:S(2)}) copy-start(bf16[2,288,512]{2,1,0:T(8,128)(2,1)} %param.5) | copy-start | bytes 1769476
  6.5 38.7 %copy-start.3 = (s32[2]{0:T(128)S(1)}, s32[2]{0:T(128)}, u32[]{:S(2)}) copy-start(s32[2]{0:T(128)} %param.6) | copy-start | bytes 28
  8.3 78.9 %copy-start.1 = (bf16[2,64,9216]{2,1,0:T(8,128)(2,1)S(1)}, bf16[2,64,9216]{2,1,0:T(8,128)(2,1)}, u32[]{:S(2)}) copy-start(bf16[2,64,9216]{2,1,0:T(8,128)(2,1)} %param.4) | copy-start | bytes 7077892
  39.6 23.8 %all-to-all-start.1 = ((bf16[32,2,8,512]{3,2,1,0:T(8,128)(2,1)}), bf16[32,2,8,512]{3,2,1,0:T(8,128)(2,1)S(1)}, u32[]{:S(2)}, u32[]{:S(2)}) async-start(bf16[32,2,8,512]{3,2,1,0:T(8,128)(2,1)} %copy.19), calls=%async_computation.1 | async-start | bytes 1048576 | tf_op jit(solution)/shard_map/all_to_all | solution.py:38
  45.1 136.6 %all-gather.6.cloned.1.call-start = ((), (), s32[]{:S(2)}) async-start(), calls=%async_computation.5 | async-start | bytes 4718592 | tf_op jit(solution)/shard_map/all_gather | solution.py:46
  87.1 181.3 %all-gather.4.cloned.1.call-start = ((), (), s32[]{:S(2)}) async-start(), calls=%async_computation.4 | async-start | bytes 9732096 | tf_op jit(solution)/shard_map/all_gather | solution.py:29
  98.6 6.5 %copy-start.2 = (s32[2,2]{1,0:T(2,128)S(1)}, s32[2,2]{1,0:T(2,128)}, u32[]{:S(2)}) copy-start(s32[2,2]{1,0:T(2,128)} %param.7) | copy-start | bytes 52
  98.6 79.3 %all-to-all-start.3 = ((bf16[32,2,64,288]{3,2,1,0:T(8,128)(2,1)}), bf16[32,2,64,288]{3,2,1,0:T(8,128)(2,1)}, u32[]{:S(2)}, u32[]{:S(2)}) async-start(bf16[32,2,64,288]{3,2,1,0:T(8,128)(2,1)} %copy.21), calls=%async_computation.3 | async-start | bytes 6291456 | tf_op jit(solution)/shard_map/all_to_all | solution.py:50
Sparse Core Ops, SparseCore 0:
  87.3 69.6 all-gather.5
  159.7 108.6 all-gather.3

commit v7 on v6

v7 whole, which is shorter than its diff:
```python
import math

import jax
import jax.numpy as jnp
from jax import lax
from jax.sharding import PartitionSpec as P


def point_positions(point_ids, offsets, panel_len):
    first = jnp.where(point_ids[None, :] // panel_len == 0, offsets[:, 0:1], offsets[:, 1:2])
    return (first + point_ids[None, :] % panel_len).astype(jnp.float32)


def local(colloc, coefficients, occupied, offsets):
    row_count = lax.axis_size(ROW)
    col_count = lax.axis_size("col")
    col_index = lax.axis_index("col")
    spin_count, own_points, basis = colloc.shape
    slots = coefficients.shape[2]
    sub_rows = own_points // col_count
    points = own_points * row_count
    panel_len = points // 2
    screen_len = panel_len // 8
    col_width = basis // col_count
    row_width = basis // row_count
    norm_factor = 1.0 / math.sqrt(points)

    own_cols = lax.dynamic_slice_in_dim(colloc, col_index * col_width, col_width, 2)
    chip_cols = lax.all_gather(own_cols, "rz", axis=1, tiled=True)
    basis_cols = lax.all_gather(chip_cols, "core", axis=0)
    core_count = basis_cols.shape[0]
    basis_cols = basis_cols.reshape(core_count, spin_count, row_count // core_count, own_points, col_width)

    own_rows = lax.dynamic_slice_in_dim(colloc, col_index * sub_rows, sub_rows, 1)
    send = own_rows.reshape(spin_count, sub_rows, row_count, row_width).transpose(2, 0, 1, 3)
    regrouped = lax.all_to_all(send, ROW, split_axis=0, concat_axis=0, tiled=True)

    partial_value = jnp.einsum(
        "xspm,smi->xspi", regrouped, coefficients, preferred_element_type=jnp.float32
    )
    received = lax.all_to_all(
        partial_value.astype(jnp.bfloat16), ROW, split_axis=0, concat_axis=0, tiled=True
    )
    summed = jnp.sum(received.astype(jnp.float32), axis=0)
    occupied_mask = jnp.arange(slots, dtype=jnp.int32)[None, :] < occupied[:, None]
    orbitals_own = jnp.where(occupied_mask[:, None, :], summed, 0.0).astype(jnp.bfloat16)
    spread = jnp.broadcast_to(orbitals_own[None], (row_count,) + orbitals_own.shape)
    orbitals_group = lax.all_to_all(spread, ROW, split_axis=0, concat_axis=0, tiled=True)
    orbitals_all = lax.all_gather(orbitals_group, "col", axis=0)
    orbitals_nat = orbitals_all.transpose(2, 1, 0, 3, 4).reshape(spin_count, points, slots)

    every = colloc.reshape(spin_count, own_points, row_count, row_width).transpose(2, 0, 1, 3)
    basis_all = lax.all_to_all(every, ROW, split_axis=0, concat_axis=0, tiled=True)
    basis_rows = jnp.moveaxis(basis_all, 1, 0).reshape(spin_count, points, row_width)

    positions = point_positions(jnp.arange(points, dtype=jnp.int32), offsets, panel_len)
    kernel = 1.0 / (1.0 + jnp.abs(positions[:, :, None] - positions[:, None, :]) / screen_len)
    density = jnp.einsum(
        "spi,sqi->spq", orbitals_nat, orbitals_nat, preferred_element_type=jnp.float32
    )
    mixed_kernel = (kernel * density / slots).astype(jnp.bfloat16)
    weighted = jnp.einsum(
        "spq,sqn->spn", mixed_kernel, basis_rows, preferred_element_type=jnp.float32
    ).astype(jnp.bfloat16)
    weighted = weighted.reshape(spin_count, row_count // core_count, core_count, own_points, -1)
    return (
        jnp.einsum("bsrjm,srbjn->msn", basis_cols, weighted, preferred_element_type=jnp.float32)
        * norm_factor
    ).astype(jnp.bfloat16)


ROW = ("rz", "core")


def solution(mesh):
    rows, cols = mesh.devices.shape
    fine = jax.sharding.Mesh(mesh.devices.reshape(rows // 2, 2, cols), ("rz", "core", "col"))
    placed = (P(None, ROW, None), P(None, ROW, None), P(), P())
    return jax.shard_map(
        local, mesh=fine, in_specs=placed, out_specs=P("col", None, ROW), check_vma=False
    )
```

time: 284 us -> 267 us (0.940)
  waiting for transfers between devices: 154 us -> 130 us
  local copies, waits for them, and re-layouts: 24.7 us -> 28.4 us
  blocking collectives: 51.7 us -> 54.8 us
    all_to_all x2, waiting for transfers between devices: 90.6 us -> 60.6 us  [the longest x1 41.3 us: local(): lax.all_to_all(every, ROW, split_axis=0, concat_axis=0, tiled=True)]
    all_gather x1, waiting for transfers between devices: 0.01 us -> 25.5 us  [local(): orbitals_all = lax.all_gather(orbitals_group, 'col', axis=0)]
    all_gather x1 -> x2, waiting for transfers between devices: 63.4 us -> 43.5 us  [the longest x1 41.9 us: local(): chip_cols = lax.all_gather(own_cols, 'rz', axis=1, tiled=True)]
    all_to_all x2, blocking collectives: 51.7 us -> 54.8 us  [the longest x1 30.5 us: local(): lax.all_to_all(send, ROW, split_axis=0, concat_axis=0, tiled=True)]
  transfers between devices with their start and end apart: 4 -> 5, of which waited for: 3 -> 5; matrix products, arithmetic and copies ran while one was open for 14% -> 17% of each run, Pallas kernels for 0% -> 0%
where the time goes in v7:
time: 267 us; the launch traced here: 266 us
  waiting for transfers between devices  130 us (49%)
  blocking collectives  54.8 us (21%)
  local copies, waits for them, and re-layouts  28.4 us (11%)
  matrix products  28.1 us (11%)
  between operations  13.2 us (5%)
  starting transfers between devices  12.1 us (5%)
    all_gather x1, waiting for transfers between devices, local(): chip_cols = lax.all_gather(own_cols, 'rz', axis=1, tiled=True)  41.9 us
    all_to_all x1, waiting for transfers between devices, local(): lax.all_to_all(every, ROW, split_axis=0, concat_axis=0, tiled=True)  41.3 us
    all_to_all x1, blocking collectives, local(): lax.all_to_all(send, ROW, split_axis=0, concat_axis=0, tiled=True)  30.5 us
    all_gather x1, waiting for transfers between devices, local(): orbitals_all = lax.all_gather(orbitals_group, 'col', axis=0)  25.5 us
    all_to_all x1, blocking collectives, local(): lax.all_to_all(spread, ROW, split_axis=0, concat_axis=0, tiled=True)  24.3 us
    all_to_all x1, waiting for transfers between devices, local(): lax.all_to_all(partial_value.astype(jnp.bfloat16), ROW, split_axis=0, con...  19.2 us
    dot_general x1, matrix products, local(): jnp.einsum('spq,sqn->spn', mixed_kernel, basis_rows, preferred_element_ty...  18.7 us
    dot_general x1, matrix products, local(): jnp.einsum('bsrjm,srbjn->msn', basis_cols, weighted, preferred_element_ty...  8.99 us
  transfers between devices with their start and end apart: 5, of which 5 were waited for; matrix products, arithmetic and copies ran while one was open for 17% of the time, Pallas kernels for 0%

profile of v7, /device:TPU:1, one launch (start us, length us, event | category | flops | bytes accessed | tf_op | source)
XLA Modules:
  0.0 266.5 jit_solution(6268526739340251166)
XLA Ops:
  6.5 1.8 constant_dynamic-slice_fusion
  8.3 1.7 constant_dynamic-slice_fusion.1
  10.0 1.7 reshape.201
  11.8 0.1 copy.29
  11.9 30.5 %all_to_all.20 = bf16[32,2,8,288]{3,2,1,0:T(8,128)(2,1)S(1)} all-to-all(bf16[32,2,8,288]{3,2,1,0:T(8,128)(2,1)S(1)} %copy.29), channel_id=1, replica_groups=mesh['rz'=16,'core'=2,'col'=8] {'rz','core'}, dimensions={0} | all-to-all | bytes 589824 | tf_op jit(solution)/shard_map/all_to_all | solution.py:36
  42.4 0.4 fusion.21
  42.8 0.9 copy.31
  43.7 5.5 %all-to-all-start.1 = ((bf16[32,2,8,512]{3,2,1,0:T(8,128)(2,1)}), bf16[32,2,8,512]{3,2,1,0:T(8,128)(2,1)S(1)}, u32[]{:S(2)}, u32[]{:S(2)}) async-start(bf16[32,2,8,512]{3,2,1,0:T(8,128)(2,1)} %copy.31), calls=%async_computation.1 | async-start | bytes 1048576 | tf_op jit(solution)/shard_map/all_to_all | solution.py:41
  49.4 19.2 %all-to-all-done.1 = bf16[32,2,8,512]{3,2,1,0:T(8,128)(2,1)S(1)} async-done(((bf16[32,2,8,512]{3,2,1,0:T(8,128)(2,1)}), bf16[32,2,8,512]{3,2,1,0:T(8,128)(2,1)S(1)}, u32[]{:S(2)}, u32[]{:S(2)}) %all-to-all-start.1) | async-done | bytes 524320 | tf_op jit(solution)/shard_map/all_to_all | solution.py:41
  68.7 24.3 %all_to_all.21 = bf16[32,2,8,512]{3,2,1,0:T(8,128)(2,1)} all-to-all(bf16[32,2,8,512]{3,2,1,0:T(8,128)(2,1)S(1)} %broadcast_in_dim.54), channel_id=1, replica_groups=mesh['rz'=16,'core'=2,'col'=8] {'rz','core'}, dimensions={0} | all-to-all | bytes 1048576 | tf_op jit(solution)/shard_map/all_to_all | solution.py:48
  93.1 5.8 %reshape.203 = bf16[2,64,32,288]{3,2,1,0:T(8,128)(2,1)} reshape(bf16[2,64,9216]{2,1,0:T(8,128)(2,1)S(1)} %copy-done.1) | data formatting | bytes 4718592 | tf_op jit(solution)/shard_map/reshape | solution.py:52
  98.8 4.7 %copy.33 = bf16[32,2,64,288]{3,2,1,0:T(8,128)(2,1)} copy(bf16[32,2,64,288]{3,0,2,1:T(8,128)(2,1)} %bitcast.40) | data formatting | bytes 4718592 | tf_op jit(solution)/shard_map/transpose | solution.py:52
  103.5 6.3 %all-to-all-start.3 = ((bf16[32,2,64,288]{3,2,1,0:T(8,128)(2,1)}), bf16[32,2,64,288]{3,2,1,0:T(8,128)(2,1)}, u32[]{:S(2)}, u32[]{:S(2)}) async-start(bf16[32,2,64,288]{3,2,1,0:T(8,128)(2,1)} %copy.33), calls=%async_computation.3 | async-start | bytes 6291456 | tf_op jit(solution)/shard_map/all_to_all | solution.py:53
  109.8 0.2 all-gather.10.cloned.1.call-start
  110.0 41.9 %all-gather.6.cloned.1.call-done = bf16[2,1024,1152]{2,1,0:T(8,128)(2,1)} async-done(((bf16[2,64,1152]{2,1,0:T(8,128)(2,1)}), bf16[2,1024,1152]{2,1,0:T(8,128)(2,1)}) %all-gather.6.cloned.1.call-update) | async-done | bytes 4718608 | tf_op jit(solution)/shard_map/all_gather | solution.py:29
  152.0 0.2 slice_reduce_fusion.1
  152.3 41.3 %all-to-all-done.3 = bf16[32,2,64,288]{3,2,1,0:T(8,128)(2,1)} async-done(((bf16[32,2,64,288]{3,2,1,0:T(8,128)(2,1)}), bf16[32,2,64,288]{3,2,1,0:T(8,128)(2,1)}, u32[]{:S(2)}, u32[]{:S(2)}) %all-to-all-start.3) | async-done | bytes 2359328 | tf_op jit(solution)/shard_map/all_to_all | solution.py:53
  193.6 4.0 %copy.34 = bf16[2,32,64,288]{3,2,1,0:T(8,128)(2,1)} copy(bf16[2,32,64,288]{3,2,0,1:T(8,128)(2,1)} %bitcast.8) | data formatting | bytes 4718592 | tf_op jit(solution)/shard_map/transpose | solution.py:54
  197.7 25.5 %all-gather.8.cloned.1.call-done = bf16[256,2,8,512]{3,2,1,0:T(8,128)(2,1)} async-done(((bf16[32,2,8,512]{3,2,1,0:T(8,128)(2,1)}), bf16[256,2,8,512]{3,2,1,0:T(8,128)(2,1)}) %all-gather.8.cloned.1.call-update) | async-done | bytes 4194320 | tf_op jit(solution)/shard_map/all_gather | solution.py:49
  223.1 4.8 %copy.32 = bf16[2,32,8,8,512]{4,3,2,1,0:T(8,128)(2,1)} copy(bf16[2,32,8,8,512]{4,3,0,1,2:T(8,128)(2,1)} %bitcast.41) | data formatting | bytes 8388608 | tf_op jit(solution)/shard_map/transpose | solution.py:50
  227.9 18.7 %fusion.15 = bf16[2,2048,288]{1,2,0:T(8,128)(2,1)S(1)} fusion(bf16[2,2048,288]{2,1,0:T(8,128)(2,1)} %bitcast.43, f32[2,2048]{1,0:T(2,128)S(1)} %add_convert_fusion, bf16[2,2048,512]{2,1,0:T(8,128)(2,1)} %bitcast.42), kind=kOutput, calls=%fused_computation.8 | convolution fusion | flops 13490061312 | bytes 8929280 | tf_op jit(solution)/shard_map/spq,sqn->spn/dot_general | solution.py:62
  246.6 2.8 %copy.36 = bf16[2,2048,288]{2,1,0:T(8,128)(2,1)} copy(bf16[2,2048,288]{1,2,0:T(8,128)(2,1)S(1)} %fusion.15) | data formatting | bytes 4718592 | tf_op jit(solution)/shard_map/convert_element_type | solution.py:64
  249.4 1.6 all-gather.10.cloned.1.call-done
  250.9 9.0 %fusion.16 = bf16[1152,2,288]{0,2,1:T(8,128)(2,1)} fusion(bf16[2,2,16,64,1152]{4,3,2,1,0:T(8,128)(2,1)} %bitcast.46, bf16[2,16,2,64,288]{4,3,2,1,0:T(8,128)(2,1)} %bitcast.44), kind=kOutput, calls=%fused_computation.9 | convolution fusion | flops 2719236096 | bytes 13123584 | tf_op jit(solution)/shard_map/bsrjm,srbjn->msn/dot_general | solution.py:67
  (20 shorter events, 0.4 us)
Async XLA Ops:
  6.5 35.8 %copy-start = (bf16[2,288,512]{2,1,0:T(8,128)(2,1)S(1)}, bf16[2,288,512]{2,1,0:T(8,128)(2,1)}, u32[]{:S(2)}) copy-start(bf16[2,288,512]{2,1,0:T(8,128)(2,1)} %param.5) | copy-start | bytes 1769476
  6.5 42.7 %copy-start.3 = (s32[2]{0:T(128)S(1)}, s32[2]{0:T(128)}, u32[]{:S(2)}) copy-start(s32[2]{0:T(128)} %param.6) | copy-start | bytes 28
  6.5 145.5 %all-gather.6.cloned.1.call-start = ((), (), s32[]{:S(2)}) async-start(), calls=%async_computation.4 | async-start | bytes 5013504 | tf_op jit(solution)/shard_map/all_gather | solution.py:29
  10.0 83.0 %copy-start.1 = (bf16[2,64,9216]{2,1,0:T(8,128)(2,1)S(1)}, bf16[2,64,9216]{2,1,0:T(8,128)(2,1)}, u32[]{:S(2)}) copy-start(bf16[2,64,9216]{2,1,0:T(8,128)(2,1)} %param.4) | copy-start | bytes 7077892
  43.7 24.9 %all-to-all-start.1 = ((bf16[32,2,8,512]{3,2,1,0:T(8,128)(2,1)}), bf16[32,2,8,512]{3,2,1,0:T(8,128)(2,1)S(1)}, u32[]{:S(2)}, u32[]{:S(2)}) async-start(bf16[32,2,8,512]{3,2,1,0:T(8,128)(2,1)} %copy.31), calls=%async_computation.1 | async-start | bytes 1048576 | tf_op jit(solution)/shard_map/all_to_all | solution.py:41
  49.2 173.9 %all-gather.8.cloned.1.call-start = ((), (), s32[]{:S(2)}) async-start(), calls=%async_computation.5 | async-start | bytes 4718592 | tf_op jit(solution)/shard_map/all_gather | solution.py:49
  103.5 48.5 %copy-start.2 = (s32[2,2]{1,0:T(2,128)S(1)}, s32[2,2]{1,0:T(2,128)}, u32[]{:S(2)}) copy-start(s32[2,2]{1,0:T(2,128)} %param.7) | copy-start | bytes 52
  103.5 90.1 %all-to-all-start.3 = ((bf16[32,2,64,288]{3,2,1,0:T(8,128)(2,1)}), bf16[32,2,64,288]{3,2,1,0:T(8,128)(2,1)}, u32[]{:S(2)}, u32[]{:S(2)}) async-start(bf16[32,2,64,288]{3,2,1,0:T(8,128)(2,1)} %copy.33), calls=%async_computation.3 | async-start | bytes 6291456 | tf_op jit(solution)/shard_map/all_to_all | solution.py:53
  109.8 141.1 %all-gather.10.cloned.1.call-start = ((), (), s32[]{:S(2)}) async-start(), calls=%async_computation.6 | async-start | bytes 14155776 | tf_op jit(solution)/shard_map/all_gather | solution.py:30
Sparse Core Ops, SparseCore 0:
  9.9 142.0 all-gather.5
  153.8 69.2 all-gather.7
  224.9 25.9 all-gather.9

commit v8 on v6

--- a/solution.py
+++ b/solution.py
@@ -9,6 +9,11 @@
 def point_positions(point_ids, offsets, panel_len):
     first = jnp.where(point_ids[None, :] // panel_len == 0, offsets[:, 0:1], offsets[:, 1:2])
     return (first + point_ids[None, :] % panel_len).astype(jnp.float32)
+
+
+def gather_col(x, col_count):
+    spread = jnp.broadcast_to(x[None], (col_count,) + x.shape)
+    return lax.all_to_all(spread, "col", split_axis=0, concat_axis=0, tiled=True)
 
 
 def local(colloc, coefficients, occupied, offsets):
@@ -43,12 +48,10 @@
     orbitals_own = jnp.where(occupied_mask[:, None, :], summed, 0.0).astype(jnp.bfloat16)
     spread = jnp.broadcast_to(orbitals_own[None], (row_count,) + orbitals_own.shape)
     orbitals_group = lax.all_to_all(spread, "row", split_axis=0, concat_axis=0, tiled=True)
-    orbitals_all = lax.all_gather(orbitals_group, "col", axis=0)
+    both = gather_col(jnp.concatenate([orbitals_group, regrouped], axis=3), col_count)
+    orbitals_all = both[..., :slots]
+    basis_rows = both[..., slots:].transpose(2, 1, 0, 3, 4).reshape(spin_count, points, row_width)
     orbitals_nat = orbitals_all.transpose(2, 1, 0, 3, 4).reshape(spin_count, points, slots)
-
-    every = colloc.reshape(spin_count, own_points, row_count, row_width).transpose(2, 0, 1, 3)
-    basis_all = lax.all_to_all(every, "row", split_axis=0, concat_axis=0, tiled=True)
-    basis_rows = jnp.moveaxis(basis_all, 1, 0).reshape(spin_count, points, row_width)
 
     positions = point_positions(jnp.arange(points, dtype=jnp.int32), offsets, panel_len)
     kernel = 1.0 / (1.0 + jnp.abs(positions[:, :, None] - positions[:, None, :]) / screen_len)

time: 284 us -> 256 us (0.901)
  the two profiles are of different devices: /device:TPU:1 before, /device:TPU:38 now
where the time goes in v8:
time: 256 us
  waiting for transfers between devices  129 us (50%)
  blocking collectives  55.6 us (22%)
  matrix products  29.8 us (12%)
  local copies, waits for them, and re-layouts  18.1 us (7%)
  between operations  13.5 us (5%)
  starting transfers between devices  9.35 us (4%)
    all_to_all x1, waiting for transfers between devices, gather_col(): lax.all_to_all(spread, 'col', split_axis=0, concat_axis=0, tiled=True)  109 us
    all_to_all x1, blocking collectives, local(): lax.all_to_all(send, 'row', split_axis=0, concat_axis=0, tiled=True)  29.6 us
    all_to_all x1, blocking collectives, local(): lax.all_to_all(spread, 'row', split_axis=0, concat_axis=0, tiled=True)  26 us
    all_to_all x1, waiting for transfers between devices, local(): lax.all_to_all(partial_value.astype(jnp.bfloat16), 'row', split_axis=0, c...  20.5 us
    dot_general x1, matrix products, local(): jnp.einsum('spq,sqn->spn', mixed_kernel, basis_rows, preferred_element_ty...  19.7 us
    dot_general x1, matrix products, local(): jnp.einsum('spm,spn->msn', basis_cols, weighted, preferred_element_type=j...  8.67 us
    all_to_all x1, starting transfers between devices, gather_col(): lax.all_to_all(spread, 'col', split_axis=0, concat_axis=0, tiled=True)  5.41 us
  transfers between devices with their start and end apart: 3, of which 2 were waited for; matrix products, arithmetic and copies ran while one was open for 15% of the time, Pallas kernels for 0%

profile of v8, /device:TPU:38, one launch (start us, length us, event | category | flops | bytes accessed | tf_op | source)
XLA Modules:
  0.0 255.8 jit_solution(694328165036783079)
XLA Ops:
  6.5 1.7 copy-done
  8.2 0.8 constant_dynamic-slice_fusion
  9.0 0.6 reshape.193
  9.6 0.1 copy.7
  9.8 29.6 %all_to_all.20 = bf16[32,2,8,288]{3,2,1,0:T(8,128)(2,1)S(1)} all-to-all(bf16[32,2,8,288]{3,2,1,0:T(8,128)(2,1)S(1)} %copy.7), channel_id=1, replica_groups=mesh['row'=32,'col'=8] {'row'}, dimensions={0} | all-to-all | bytes 589824 | tf_op jit(solution)/shard_map/all_to_all | solution.py:38
  39.4 1.5 fusion.4
  40.9 0.9 copy.9
  41.7 3.9 %all-to-all-start.1 = ((bf16[32,2,8,512]{3,2,1,0:T(8,128)(2,1)}), bf16[32,2,8,512]{3,2,1,0:T(8,128)(2,1)S(1)}, u32[]{:S(2)}, u32[]{:S(2)}) async-start(bf16[32,2,8,512]{3,2,1,0:T(8,128)(2,1)} %copy.9), calls=%async_computation.1 | async-start | bytes 1048576 | tf_op jit(solution)/shard_map/all_to_all | solution.py:43
  45.8 20.5 %all-to-all-done.1 = bf16[32,2,8,512]{3,2,1,0:T(8,128)(2,1)S(1)} async-done(((bf16[32,2,8,512]{3,2,1,0:T(8,128)(2,1)}), bf16[32,2,8,512]{3,2,1,0:T(8,128)(2,1)S(1)}, u32[]{:S(2)}, u32[]{:S(2)}) %all-to-all-start.1) | async-done | bytes 524320 | tf_op jit(solution)/shard_map/all_to_all | solution.py:43
  66.3 0.1 convert_reduce_fusion
  66.4 26.0 %all_to_all.21 = bf16[32,2,8,512]{3,2,1,0:T(8,128)(2,1)S(1)} all-to-all(bf16[32,2,8,512]{3,2,1,0:T(8,128)(2,1)S(1)} %broadcast_in_dim.60), channel_id=1, replica_groups=mesh['row'=32,'col'=8] {'row'}, dimensions={0} | all-to-all | bytes 1048576 | tf_op jit(solution)/shard_map/all_to_all | solution.py:50
  92.4 0.1 pad_maximum_fusion
  92.5 0.1 copy.10
  92.6 4.0 %broadcast_in_dim.61 = bf16[8,32,2,8,800]{4,3,1,2,0:T(8,128)(2,1)} broadcast(bf16[32,2,8,800]{3,2,0,1:T(8,128)(2,1)S(1)} %copy.10), dimensions={1,2,3,4} | broadcast | bytes 7372800 | tf_op jit(solution)/shard_map/broadcast_in_dim | solution.py:15
  96.6 5.4 %all-to-all-start.3 = ((bf16[8,32,2,8,800]{4,3,1,2,0:T(8,128)(2,1)}), bf16[8,32,2,8,800]{4,3,1,2,0:T(8,128)(2,1)}, u32[]{:S(2)}, u32[]{:S(2)}) async-start(bf16[8,32,2,8,800]{4,3,1,2,0:T(8,128)(2,1)} %broadcast_in_dim.61), calls=%async_computation.3 | async-start | bytes 14680064 | tf_op jit(solution)/shard_map/all_to_all | solution.py:16
  102.0 0.2 slice_reduce_fusion.1
  102.2 0.1 add_convert_fusion
  102.3 108.6 %all-to-all-done.3 = bf16[8,32,2,8,800]{4,3,1,2,0:T(8,128)(2,1)} async-done(((bf16[8,32,2,8,800]{4,3,1,2,0:T(8,128)(2,1)}), bf16[8,32,2,8,800]{4,3,1,2,0:T(8,128)(2,1)}, u32[]{:S(2)}, u32[]{:S(2)}) %all-to-all-start.3) | async-done | bytes 6553632 | tf_op jit(solution)/shard_map/all_to_all | solution.py:16
  210.8 2.3 slice_bitcast_fusion
  213.1 2.2 copy.12
  215.4 2.6 %slice.22 = bf16[8,32,2,8,512]{4,3,1,2,0:T(8,128)(2,1)S(1)} slice(bf16[8,32,2,8,800]{4,3,1,2,0:T(8,128)(2,1)} %all-to-all-done.3), slice={[0:8], [0:32], [0:2], [0:8], [0:512]} | slice | bytes 8388608 | tf_op jit(solution)/shard_map/slice | solution.py:52
  218.0 2.7 %copy.16 = bf16[8,32,2,8,512]{4,3,0,1,2:T(8,128)(2,1)} copy(bf16[8,32,2,8,512]{4,3,1,2,0:T(8,128)(2,1)S(1)} %slice.22) | data formatting | bytes 8388608
  220.7 19.7 %fusion.1 = bf16[2,2048,288]{1,2,0:T(8,128)(2,1)} fusion(bf16[2,2048,288]{2,1,0:T(8,128)(2,1)} %bitcast.30, f32[2,2048]{1,0:T(2,128)S(1)} %add_convert_fusion, bf16[2,2048,512]{2,1,0:T(8,128)(2,1)} %bitcast.29), kind=kOutput, calls=%fused_computation.4 | convolution fusion | flops 13490061312 | bytes 8929280 | tf_op jit(solution)/shard_map/spq,sqn->spn/dot_general | solution.py:62
  240.3 8.7 %fusion.3 = bf16[1152,2,288]{0,2,1:T(8,128)(2,1)} fusion(bf16[2,2048,288]{1,2,0:T(8,128)(2,1)} %fusion.1, bf16[2,2048,1152]{2,1,0:T(8,128)(2,1)} %all-gather.2.cloned.1.call-done), kind=kOutput, calls=%fused_computation.6 | convolution fusion | flops 2719236096 | bytes 13123584 | tf_op jit(solution)/shard_map/spm,spn->msn/dot_general | solution.py:66
  (14 shorter events, 0.2 us)
Async XLA Ops:
  6.5 1.7 copy-start
  6.5 39.2 %copy-start.2 = (s32[2]{0:T(128)S(1)}, s32[2]{0:T(128)}, u32[]{:S(2)}) copy-start(s32[2]{0:T(128)} %param.6) | copy-start | bytes 28
  6.5 233.8 %all-gather.2.cloned.1.call-start = ((), (), s32[]{:S(2)}) async-start(), calls=%async_computation.4 | async-start | bytes 9732096 | tf_op jit(solution)/shard_map/all_gather | solution.py:34
  41.7 24.5 %all-to-all-start.1 = ((bf16[32,2,8,512]{3,2,1,0:T(8,128)(2,1)}), bf16[32,2,8,512]{3,2,1,0:T(8,128)(2,1)S(1)}, u32[]{:S(2)}, u32[]{:S(2)}) async-start(bf16[32,2,8,512]{3,2,1,0:T(8,128)(2,1)} %copy.9), calls=%async_computation.1 | async-start | bytes 1048576 | tf_op jit(solution)/shard_map/all_to_all | solution.py:43
  96.6 5.4 %copy-start.1 = (s32[2,2]{1,0:T(2,128)S(1)}, s32[2,2]{1,0:T(2,128)}, u32[]{:S(2)}) copy-start(s32[2,2]{1,0:T(2,128)} %param.7) | copy-start | bytes 52
  96.6 114.3 %all-to-all-start.3 = ((bf16[8,32,2,8,800]{4,3,1,2,0:T(8,128)(2,1)}), bf16[8,32,2,8,800]{4,3,1,2,0:T(8,128)(2,1)}, u32[]{:S(2)}, u32[]{:S(2)}) async-start(bf16[8,32,2,8,800]{4,3,1,2,0:T(8,128)(2,1)} %broadcast_in_dim.61), calls=%async_computation.3 | async-start | bytes 14680064 | tf_op jit(solution)/shard_map/all_to_all | solution.py:16
Sparse Core Ops, SparseCore 0:
  10.1 141.9 all-gather.1

commit v9 on v8

--- a/solution.py
+++ b/solution.py
@@ -36,6 +36,8 @@
     own_rows = lax.dynamic_slice_in_dim(colloc, col_index * sub_rows, sub_rows, 1)
     send = own_rows.reshape(spin_count, sub_rows, row_count, row_width).transpose(2, 0, 1, 3)
     regrouped = lax.all_to_all(send, "row", split_axis=0, concat_axis=0, tiled=True)
+    basis_all = lax.all_gather(regrouped, "col", axis=0)
+    basis_rows = basis_all.transpose(2, 1, 0, 3, 4).reshape(spin_count, points, row_width)
 
     partial_value = jnp.einsum(
         "xspm,smi->xspi", regrouped, coefficients, preferred_element_type=jnp.float32
@@ -48,9 +50,7 @@
     orbitals_own = jnp.where(occupied_mask[:, None, :], summed, 0.0).astype(jnp.bfloat16)
     spread = jnp.broadcast_to(orbitals_own[None], (row_count,) + orbitals_own.shape)
     orbitals_group = lax.all_to_all(spread, "row", split_axis=0, concat_axis=0, tiled=True)
-    both = gather_col(jnp.concatenate([orbitals_group, regrouped], axis=3), col_count)
-    orbitals_all = both[..., :slots]
-    basis_rows = both[..., slots:].transpose(2, 1, 0, 3, 4).reshape(spin_count, points, row_width)
+    orbitals_all = gather_col(orbitals_group, col_count)
     orbitals_nat = orbitals_all.transpose(2, 1, 0, 3, 4).reshape(spin_count, points, slots)
 
     positions = point_positions(jnp.arange(points, dtype=jnp.int32), offsets, panel_len)

time: 256 us -> 232 us (0.906)
  the two profiles are of different devices: /device:TPU:38 before, /device:TPU:1 now
where the time goes in v9:
time: 232 us; the launch traced here: 228 us
  waiting for transfers between devices  106 us (46%)
  blocking collectives  52.7 us (23%)
  matrix products  29.9 us (13%)
  local copies, waits for them, and re-layouts  15.6 us (7%)
  between operations  13.5 us (6%)
  starting transfers between devices  10.5 us (5%)
    all_to_all x1, waiting for transfers between devices, gather_col(): lax.all_to_all(spread, 'col', split_axis=0, concat_axis=0, tiled=True)  45 us
    all_to_all x1, waiting for transfers between devices, local(): lax.all_to_all(partial_value.astype(jnp.bfloat16), 'row', split_axis=0, c...  38.7 us
    all_to_all x1, blocking collectives, local(): lax.all_to_all(send, 'row', split_axis=0, concat_axis=0, tiled=True)  28.2 us
    all_to_all x1, blocking collectives, local(): lax.all_to_all(spread, 'row', split_axis=0, concat_axis=0, tiled=True)  24.5 us
    all_gather x1, waiting for transfers between devices, local(): basis_cols = lax.all_gather(own_cols, 'row', axis=1, tiled=True)  22.2 us
    dot_general x1, matrix products, local(): jnp.einsum('spq,sqn->spn', mixed_kernel, basis_rows, preferred_element_ty...  19.6 us
    dot_general x1, matrix products, local(): jnp.einsum('spm,spn->msn', basis_cols, weighted, preferred_element_type=j...  8.67 us
    all_to_all x1, starting transfers between devices, local(): lax.all_to_all(partial_value.astype(jnp.bfloat16), 'row', split_axis=0, c...  5.56 us
  transfers between devices with their start and end apart: 4, of which 3 were waited for; matrix products, arithmetic and copies ran while one was open for 15% of the time, Pallas kernels for 0%

profile of v9, /device:TPU:1, one launch (start us, length us, event | category | flops | bytes accessed | tf_op | source)
XLA Modules:
  0.0 228.3 jit_solution(13062598325515934451)
XLA Ops:
  6.5 1.7 copy-done
  8.2 0.6 reshape.193
  8.8 0.1 copy.14
  9.0 28.2 %all_to_all.20 = bf16[32,2,8,288]{3,2,1,0:T(8,128)(2,1)} all-to-all(bf16[32,2,8,288]{3,2,1,0:T(8,128)(2,1)S(1)} %copy.14), channel_id=1, replica_groups=mesh['row'=32,'col'=8] {'row'}, dimensions={0} | all-to-all | bytes 589824 | tf_op jit(solution)/shard_map/all_to_all | solution.py:38
  37.2 0.0 all-gather.4.cloned.1.call-start
  37.3 0.7 constant_dynamic-slice_fusion
  38.0 1.6 fusion.4
  39.7 0.9 copy.16
  40.5 5.6 %all-to-all-start.1 = ((bf16[32,2,8,512]{3,2,1,0:T(8,128)(2,1)}), bf16[32,2,8,512]{3,2,1,0:T(8,128)(2,1)S(1)}, u32[]{:S(2)}, u32[]{:S(2)}) async-start(bf16[32,2,8,512]{3,2,1,0:T(8,128)(2,1)} %copy.16), calls=%async_computation.1 | async-start | bytes 1048576 | tf_op jit(solution)/shard_map/all_to_all | solution.py:45
  46.1 0.1 iota_compare_fusion
  46.2 38.7 %all-to-all-done.1 = bf16[32,2,8,512]{3,2,1,0:T(8,128)(2,1)S(1)} async-done(((bf16[32,2,8,512]{3,2,1,0:T(8,128)(2,1)}), bf16[32,2,8,512]{3,2,1,0:T(8,128)(2,1)S(1)}, u32[]{:S(2)}, u32[]{:S(2)}) %all-to-all-start.1) | async-done | bytes 524320 | tf_op jit(solution)/shard_map/all_to_all | solution.py:45
  84.8 0.1 convert_reduce_fusion
  84.9 0.1 broadcast_in_dim.60
  85.0 24.5 %all_to_all.21 = bf16[32,2,8,512]{3,2,1,0:T(8,128)(2,1)S(1)} all-to-all(bf16[32,2,8,512]{3,2,1,0:T(8,128)(2,1)S(1)} %broadcast_in_dim.60), channel_id=1, replica_groups=mesh['row'=32,'col'=8] {'row'}, dimensions={0} | all-to-all | bytes 1048576 | tf_op jit(solution)/shard_map/all_to_all | solution.py:52
  109.5 2.4 %broadcast_in_dim.61 = bf16[8,32,2,8,512]{4,3,1,2,0:T(8,128)(2,1)} broadcast(bf16[32,2,8,512]{3,2,0,1:T(8,128)(2,1)S(1)} %copy.17), dimensions={1,2,3,4} | broadcast | bytes 4718592 | tf_op jit(solution)/shard_map/broadcast_in_dim | solution.py:15
  111.9 4.8 %all-to-all-start.3 = ((bf16[8,32,2,8,512]{4,3,1,2,0:T(8,128)(2,1)}), bf16[8,32,2,8,512]{4,3,1,2,0:T(8,128)(2,1)}, u32[]{:S(2)}, u32[]{:S(2)}) async-start(bf16[8,32,2,8,512]{4,3,1,2,0:T(8,128)(2,1)} %broadcast_in_dim.61), calls=%async_computation.3 | async-start | bytes 8388608 | tf_op jit(solution)/shard_map/all_to_all | solution.py:16
  116.7 0.2 slice_reduce_fusion.1
  116.9 0.1 add_convert_fusion
  117.0 4.2 %copy.19 = bf16[8,32,2,8,288]{4,3,0,1,2:T(8,128)(2,1)} copy(bf16[8,32,2,8,288]{4,3,2,1,0:T(8,128)(2,1)} %bitcast.31) | data formatting | bytes 4718592 | tf_op jit(solution)/shard_map/all_gather | solution.py:39
  121.2 45.0 %all-to-all-done.3 = bf16[8,32,2,8,512]{4,3,1,2,0:T(8,128)(2,1)} async-done(((bf16[8,32,2,8,512]{4,3,1,2,0:T(8,128)(2,1)}), bf16[8,32,2,8,512]{4,3,1,2,0:T(8,128)(2,1)}, u32[]{:S(2)}, u32[]{:S(2)}) %all-to-all-start.3) | async-done | bytes 4194336 | tf_op jit(solution)/shard_map/all_to_all | solution.py:16
  166.2 4.8 %copy.18 = bf16[8,32,2,8,512]{4,3,0,1,2:T(8,128)(2,1)} copy(bf16[8,32,2,8,512]{4,3,1,2,0:T(8,128)(2,1)} %all-to-all-done.3) | data formatting | bytes 8388608 | tf_op jit(solution)/shard_map/all_to_all | solution.py:16
  170.9 19.6 %fusion.1 = bf16[2,2048,288]{1,2,0:T(8,128)(2,1)} fusion(bf16[2,2048,288]{2,1,0:T(8,128)(2,1)} %bitcast.32, f32[2,2048]{1,0:T(2,128)S(1)} %add_convert_fusion, bf16[2,2048,512]{2,1,0:T(8,128)(2,1)} %bitcast.30), kind=kOutput, calls=%fused_computation.3 | convolution fusion | flops 13490061312 | bytes 8929280 | tf_op jit(solution)/shard_map/spq,sqn->spn/dot_general | solution.py:62
  190.5 22.2 %all-gather.4.cloned.1.call-done = bf16[2,2048,1152]{2,1,0:T(8,128)(2,1)} async-done(((bf16[2,64,1152]{2,1,0:T(8,128)(2,1)}), bf16[2,2048,1152]{2,1,0:T(8,128)(2,1)}) %all-gather.4.cloned.1.call-update) | async-done | bytes 9437200 | tf_op jit(solution)/shard_map/all_gather | solution.py:34
  212.8 8.7 %fusion.3 = bf16[1152,2,288]{0,2,1:T(8,128)(2,1)} fusion(bf16[2,2048,288]{1,2,0:T(8,128)(2,1)} %fusion.1, bf16[2,2048,1152]{2,1,0:T(8,128)(2,1)} %all-gather.4.cloned.1.call-done), kind=kOutput, calls=%fused_computation.5 | convolution fusion | flops 2719236096 | bytes 13123584 | tf_op jit(solution)/shard_map/spm,spn->msn/dot_general | solution.py:66
  (14 shorter events, 0.1 us)
Async XLA Ops:
  6.5 1.7 copy-start
  6.5 39.6 %copy-start.2 = (s32[2]{0:T(128)S(1)}, s32[2]{0:T(128)}, u32[]{:S(2)}) copy-start(s32[2]{0:T(128)} %param.6) | copy-start | bytes 28
  6.5 110.5 %all-gather.6.cloned.1.call-start = ((), (), s32[]{:S(2)}) async-start(), calls=%async_computation.5 | async-start | bytes 3538944 | tf_op jit(solution)/shard_map/all_gather | solution.py:39
  37.2 175.6 %all-gather.4.cloned.1.call-start = ((), (), s32[]{:S(2)}) async-start(), calls=%async_computation.4 | async-start | bytes 9732096 | tf_op jit(solution)/shard_map/all_gather | solution.py:34
  40.5 44.3 %all-to-all-start.1 = ((bf16[32,2,8,512]{3,2,1,0:T(8,128)(2,1)}), bf16[32,2,8,512]{3,2,1,0:T(8,128)(2,1)S(1)}, u32[]{:S(2)}, u32[]{:S(2)}) async-start(bf16[32,2,8,512]{3,2,1,0:T(8,128)(2,1)} %copy.16), calls=%async_computation.1 | async-start | bytes 1048576 | tf_op jit(solution)/shard_map/all_to_all | solution.py:45
  111.9 4.9 %copy-start.1 = (s32[2,2]{1,0:T(2,128)S(1)}, s32[2,2]{1,0:T(2,128)}, u32[]{:S(2)}) copy-start(s32[2,2]{1,0:T(2,128)} %param.7) | copy-start | bytes 52
  111.9 54.3 %all-to-all-start.3 = ((bf16[8,32,2,8,512]{4,3,1,2,0:T(8,128)(2,1)}), bf16[8,32,2,8,512]{4,3,1,2,0:T(8,128)(2,1)}, u32[]{:S(2)}, u32[]{:S(2)}) async-start(bf16[8,32,2,8,512]{4,3,1,2,0:T(8,128)(2,1)} %broadcast_in_dim.61), calls=%async_computation.3 | async-start | bytes 8388608 | tf_op jit(solution)/shard_map/all_to_all | solution.py:16
Sparse Core Ops, SparseCore 0:
  37.3 44.7 all-gather.5
  85.0 127.7 all-gather.3

commit v10 on v9

--- a/solution.py
+++ b/solution.py
@@ -36,7 +36,7 @@
     own_rows = lax.dynamic_slice_in_dim(colloc, col_index * sub_rows, sub_rows, 1)
     send = own_rows.reshape(spin_count, sub_rows, row_count, row_width).transpose(2, 0, 1, 3)
     regrouped = lax.all_to_all(send, "row", split_axis=0, concat_axis=0, tiled=True)
-    basis_all = lax.all_gather(regrouped, "col", axis=0)
+    basis_all = gather_col(regrouped, col_count)
     basis_rows = basis_all.transpose(2, 1, 0, 3, 4).reshape(spin_count, points, row_width)
 
     partial_value = jnp.einsum(
@@ -50,7 +50,9 @@
     orbitals_own = jnp.where(occupied_mask[:, None, :], summed, 0.0).astype(jnp.bfloat16)
     spread = jnp.broadcast_to(orbitals_own[None], (row_count,) + orbitals_own.shape)
     orbitals_group = lax.all_to_all(spread, "row", split_axis=0, concat_axis=0, tiled=True)
-    orbitals_all = gather_col(orbitals_group, col_count)
+    orbitals_first = gather_col(orbitals_group[:, :1], col_count)
+    orbitals_rest = lax.all_gather(orbitals_group[:, 1:], "col", axis=0)
+    orbitals_all = jnp.concatenate([orbitals_first, orbitals_rest], axis=2)
     orbitals_nat = orbitals_all.transpose(2, 1, 0, 3, 4).reshape(spin_count, points, slots)
 
     positions = point_positions(jnp.arange(points, dtype=jnp.int32), offsets, panel_len)

time: 232 us -> 281 us (1.21); the launches traced: 228 us -> 281 us
  blocking collectives: 52.7 us -> 109 us
  waiting for transfers between devices: 106 us -> 102 us
    all_to_all x0 -> x1, blocking collectives: none -> 57.9 us  [gather_col(): lax.all_to_all(spread, 'col', split_axis=0, concat_axis=0, tiled=True)]
    all_gather x1, waiting for transfers between devices: 22.2 us -> 60.7 us  [local(): basis_cols = lax.all_gather(own_cols, 'row', axis=1, tiled=True)]
    all_to_all x1, waiting for transfers between devices: 45 us -> 22.7 us  [gather_col(): lax.all_to_all(spread, 'col', split_axis=0, concat_axis=0, tiled=True)]
    all_to_all x1, waiting for transfers between devices: 38.7 us -> 18.1 us  [local(): lax.all_to_all(partial_value.astype(jnp.bfloat16), 'row', split_axis=0, c...]
    transpose x0 -> x2, local copies, waits for them, and re-layouts: none -> 6.8 us  [the longest x1 4.21 us: local(): basis_all.transpose(2, 1, 0, 3, 4).reshape(spin_count, points, row_width)]
    all_to_all x2 -> x1, local copies, waits for them, and re-layouts: 4.79 us -> 0.04 us  [local(): lax.all_to_all(send, 'row', split_axis=0, concat_axis=0, tiled=True)]
    all_gather x1 -> x0, local copies, waits for them, and re-layouts: 4.16 us -> none  [local(): basis_all = lax.all_gather(regrouped, 'col', axis=0)]
  transfers between devices with their start and end apart: 4 -> 4, of which waited for: 3 -> 3; matrix products, arithmetic and copies ran while one was open for 15% -> 11% of each run, Pallas kernels for 0% -> 0%
where the time goes in v10:
time: 281 us
  blocking collectives  109 us (39%)
  waiting for transfers between devices  102 us (36%)
  matrix products  29.7 us (11%)
  local copies, waits for them, and re-layouts  13.8 us (5%)
  between operations  13.5 us (5%)
  starting transfers between devices  10.4 us (4%)
  other arithmetic  2.88 us (1%)
    all_gather x1, waiting for transfers between devices, local(): basis_cols = lax.all_gather(own_cols, 'row', axis=1, tiled=True)  60.7 us
    all_to_all x1, blocking collectives, gather_col(): lax.all_to_all(spread, 'col', split_axis=0, concat_axis=0, tiled=True)  57.9 us
    all_to_all x1, blocking collectives, local(): lax.all_to_all(send, 'row', split_axis=0, concat_axis=0, tiled=True)  28.1 us
    all_to_all x1, blocking collectives, local(): lax.all_to_all(spread, 'row', split_axis=0, concat_axis=0, tiled=True)  22.9 us
    all_to_all x1, waiting for transfers between devices, gather_col(): lax.all_to_all(spread, 'col', split_axis=0, concat_axis=0, tiled=True)  22.7 us
    dot_general x1, matrix products, local(): jnp.einsum('spq,sqn->spn', mixed_kernel, basis_rows, preferred_element_ty...  19.5 us
    all_to_all x1, waiting for transfers between devices, local(): lax.all_to_all(partial_value.astype(jnp.bfloat16), 'row', split_axis=0, c...  18.1 us
    dot_general x1, matrix products, local(): jnp.einsum('spm,spn->msn', basis_cols, weighted, preferred_element_type=j...  8.67 us
  transfers between devices with their start and end apart: 4, of which 3 were waited for; matrix products, arithmetic and copies ran while one was open for 11% of the time, Pallas kernels for 0%

profile of v10, /device:TPU:1, one launch (start us, length us, event | category | flops | bytes accessed | tf_op | source)
XLA Modules:
  0.0 280.7 jit_solution(7257025805138158793)
XLA Ops:
  6.5 1.7 copy-done
  8.2 0.6 reshape.196
  8.8 0.1 copy.10
  9.0 28.1 %all_to_all.25 = bf16[32,2,8,288]{3,2,1,0:T(8,128)(2,1)S(1)} all-to-all(bf16[32,2,8,288]{3,2,1,0:T(8,128)(2,1)S(1)} %copy.10), channel_id=1, replica_groups=mesh['row'=32,'col'=8] {'row'}, dimensions={0} | all-to-all | bytes 589824 | tf_op jit(solution)/shard_map/all_to_all | solution.py:38
  37.1 1.5 fusion.4
  38.6 0.9 copy.12
  39.5 5.6 %all-to-all-start.1 = ((bf16[32,2,8,512]{3,2,1,0:T(8,128)(2,1)}), bf16[32,2,8,512]{3,2,1,0:T(8,128)(2,1)S(1)}, u32[]{:S(2)}, u32[]{:S(2)}) async-start(bf16[32,2,8,512]{3,2,1,0:T(8,128)(2,1)} %copy.12), calls=%async_computation.1 | async-start | bytes 1048576 | tf_op jit(solution)/shard_map/all_to_all | solution.py:45
  45.2 18.1 %all-to-all-done.1 = bf16[32,2,8,512]{3,2,1,0:T(8,128)(2,1)S(1)} async-done(((bf16[32,2,8,512]{3,2,1,0:T(8,128)(2,1)}), bf16[32,2,8,512]{3,2,1,0:T(8,128)(2,1)S(1)}, u32[]{:S(2)}, u32[]{:S(2)}) %all-to-all-start.1) | async-done | bytes 524320 | tf_op jit(solution)/shard_map/all_to_all | solution.py:45
  63.2 0.1 convert_reduce_fusion
  63.4 22.9 %all_to_all.26 = bf16[32,2,8,512]{3,2,1,0:T(8,128)(2,1)S(1)} all-to-all(bf16[32,2,8,512]{3,2,1,0:T(8,128)(2,1)S(1)} %broadcast_in_dim.68), channel_id=1, replica_groups=mesh['row'=32,'col'=8] {'row'}, dimensions={0} | all-to-all | bytes 1048576 | tf_op jit(solution)/shard_map/all_to_all | solution.py:52
  86.3 0.7 slice_bitcast_fusion
  87.1 0.7 constant_dynamic-slice_fusion
  88.0 0.4 broadcast_in_dim.71
  88.4 57.9 %all_to_all.27 = bf16[8,32,2,8,288]{4,3,1,2,0:T(8,128)(2,1)} all-to-all(bf16[8,32,2,8,288]{4,3,1,2,0:T(8,128)(2,1)S(1)} %broadcast_in_dim.71), channel_id=1, replica_groups=mesh['row'=32,'col'=8] {'col'}, dimensions={0} | all-to-all | bytes 4718592 | tf_op jit(solution)/shard_map/all_to_all | solution.py:16
  146.3 1.5 broadcast_in_dim.70
  147.8 4.8 %all-to-all-start.3 = ((bf16[8,32,1,8,512]{4,3,1,2,0:T(8,128)(2,1)}), bf16[8,32,1,8,512]{4,3,1,2,0:T(8,128)(2,1)}, u32[]{:S(2)}, u32[]{:S(2)}) async-start(bf16[8,32,1,8,512]{4,3,1,2,0:T(8,128)(2,1)} %broadcast_in_dim.70), calls=%async_computation.3 | async-start | bytes 4194304 | tf_op jit(solution)/shard_map/all_to_all | solution.py:16
  152.6 0.2 slice_reduce_fusion.1
  152.9 4.2 %copy.16 = bf16[2,32,8,8,288]{4,3,2,1,0:T(8,128)(2,1)} copy(bf16[2,32,8,8,288]{4,3,1,0,2:T(8,128)(2,1)} %bitcast.32) | data formatting | bytes 4718592 | tf_op jit(solution)/shard_map/transpose | solution.py:40
  157.1 22.7 %all-to-all-done.3 = bf16[8,32,1,8,512]{4,3,1,2,0:T(8,128)(2,1)} async-done(((bf16[8,32,1,8,512]{4,3,1,2,0:T(8,128)(2,1)}), bf16[8,32,1,8,512]{4,3,1,2,0:T(8,128)(2,1)}, u32[]{:S(2)}, u32[]{:S(2)}) %all-to-all-start.3) | async-done | bytes 2097184 | tf_op jit(solution)/shard_map/all_to_all | solution.py:16
  179.8 2.6 maximum_bitcast_fusion
  182.4 2.6 copy.14
  185.0 19.5 %fusion.1 = bf16[2,2048,288]{1,2,0:T(8,128)(2,1)} fusion(bf16[2,2048,288]{2,1,0:T(8,128)(2,1)} %bitcast.34, f32[2,2048]{1,0:T(2,128)S(1)} %add_convert_fusion, bf16[2,2048,512]{2,1,0:T(8,128)(2,1)} %bitcast.33), kind=kOutput, calls=%fused_computation.4 | convolution fusion | flops 13490061312 | bytes 8929280 | tf_op jit(solution)/shard_map/spq,sqn->spn/dot_general | solution.py:64
  204.5 60.7 %all-gather.4.cloned.1.call-done = bf16[2,2048,1152]{2,1,0:T(8,128)(2,1)} async-done(((bf16[2,64,1152]{2,1,0:T(8,128)(2,1)}), bf16[2,2048,1152]{2,1,0:T(8,128)(2,1)}) %all-gather.4.cloned.1.call-update) | async-done | bytes 9437200 | tf_op jit(solution)/shard_map/all_gather | solution.py:34
  265.2 8.7 %fusion.3 = bf16[1152,2,288]{0,2,1:T(8,128)(2,1)} fusion(bf16[2,2048,288]{1,2,0:T(8,128)(2,1)} %fusion.1, bf16[2,2048,1152]{2,1,0:T(8,128)(2,1)} %all-gather.4.cloned.1.call-done), kind=kOutput, calls=%fused_computation.6 | convolution fusion | flops 2719236096 | bytes 13123584 | tf_op jit(solution)/shard_map/spm,spn->msn/dot_general | solution.py:68
  (18 shorter events, 0.4 us)
Async XLA Ops:
  6.5 1.7 copy-start
  6.5 38.5 %copy-start.2 = (s32[2]{0:T(128)S(1)}, s32[2]{0:T(128)}, u32[]{:S(2)}) copy-start(s32[2]{0:T(128)} %param.6) | copy-start | bytes 28
  39.5 23.8 %all-to-all-start.1 = ((bf16[32,2,8,512]{3,2,1,0:T(8,128)(2,1)}), bf16[32,2,8,512]{3,2,1,0:T(8,128)(2,1)S(1)}, u32[]{:S(2)}, u32[]{:S(2)}) async-start(bf16[32,2,8,512]{3,2,1,0:T(8,128)(2,1)} %copy.12), calls=%async_computation.1 | async-start | bytes 1048576 | tf_op jit(solution)/shard_map/all_to_all | solution.py:45
  45.0 134.8 %all-gather.6.cloned.1.call-start = ((), (), s32[]{:S(2)}) async-start(), calls=%async_computation.6 | async-start | bytes 2359296 | tf_op jit(solution)/shard_map/all_gather | solution.py:54
  87.1 178.2 %all-gather.4.cloned.1.call-start = ((), (), s32[]{:S(2)}) async-start(), calls=%async_computation.5 | async-start | bytes 9732096 | tf_op jit(solution)/shard_map/all_gather | solution.py:34
  146.3 6.3 %copy-start.1 = (s32[2,2]{1,0:T(2,128)S(1)}, s32[2,2]{1,0:T(2,128)}, u32[]{:S(2)}) copy-start(s32[2,2]{1,0:T(2,128)} %param.7) | copy-start | bytes 52
  147.8 32.0 %all-to-all-start.3 = ((bf16[8,32,1,8,512]{4,3,1,2,0:T(8,128)(2,1)}), bf16[8,32,1,8,512]{4,3,1,2,0:T(8,128)(2,1)}, u32[]{:S(2)}, u32[]{:S(2)}) async-start(bf16[8,32,1,8,512]{4,3,1,2,0:T(8,128)(2,1)} %broadcast_in_dim.70), calls=%async_computation.3 | async-start | bytes 4194304 | tf_op jit(solution)/shard_map/all_to_all | solution.py:16
Sparse Core Ops, SparseCore 0:
  87.2 63.8 all-gather.5
  153.9 111.3 all-gather.3

commit v11 on v10

--- a/solution.py
+++ b/solution.py
@@ -52,22 +52,26 @@
     orbitals_group = lax.all_to_all(spread, "row", split_axis=0, concat_axis=0, tiled=True)
     orbitals_first = gather_col(orbitals_group[:, :1], col_count)
     orbitals_rest = lax.all_gather(orbitals_group[:, 1:], "col", axis=0)
-    orbitals_all = jnp.concatenate([orbitals_first, orbitals_rest], axis=2)
-    orbitals_nat = orbitals_all.transpose(2, 1, 0, 3, 4).reshape(spin_count, points, slots)
 
     positions = point_positions(jnp.arange(points, dtype=jnp.int32), offsets, panel_len)
     kernel = 1.0 / (1.0 + jnp.abs(positions[:, :, None] - positions[:, None, :]) / screen_len)
-    density = jnp.einsum(
-        "spi,sqi->spq", orbitals_nat, orbitals_nat, preferred_element_type=jnp.float32
-    )
-    mixed_kernel = (kernel * density / slots).astype(jnp.bfloat16)
-    weighted = jnp.einsum(
-        "spq,sqn->spn", mixed_kernel, basis_rows, preferred_element_type=jnp.float32
-    ).astype(jnp.bfloat16)
-    return (
-        jnp.einsum("spm,spn->msn", basis_cols, weighted, preferred_element_type=jnp.float32)
-        * norm_factor
-    ).astype(jnp.bfloat16)
+    blocks = []
+    for spin, orbitals_all in enumerate((orbitals_first, orbitals_rest)):
+        orbitals_nat = orbitals_all[:, :, 0].transpose(1, 0, 2, 3).reshape(points, slots)
+        density = jnp.einsum(
+            "pi,qi->pq", orbitals_nat, orbitals_nat, preferred_element_type=jnp.float32
+        )
+        mixed_kernel = (kernel[spin] * density / slots).astype(jnp.bfloat16)
+        weighted = jnp.einsum(
+            "pq,qn->pn", mixed_kernel, basis_rows[spin], preferred_element_type=jnp.float32
+        ).astype(jnp.bfloat16)
+        blocks.append(
+            (
+                jnp.einsum("pm,pn->mn", basis_cols[spin], weighted, preferred_element_type=jnp.float32)
+                * norm_factor
+            ).astype(jnp.bfloat16)
+        )
+    return jnp.stack(blocks, axis=1)
 
 
 def solution(mesh):

time: 281 us -> 301 us (1.071)
  blocking collectives: 109 us -> 51 us
  waiting for transfers between devices: 102 us -> 145 us
  starting transfers between devices: 10.4 us -> 24.3 us
  other arithmetic: 2.88 us -> 13 us
  matrix products: 29.7 us -> 35.2 us
  local copies, waits for them, and re-layouts: 13.8 us -> 18.2 us
    all_to_all x1 -> x0, blocking collectives: 57.9 us -> none  [gather_col(): lax.all_to_all(spread, 'col', split_axis=0, concat_axis=0, tiled=True)]
    all_to_all x1 -> x2, waiting for transfers between devices: 22.7 us -> 61.4 us  [gather_col(): lax.all_to_all(spread, 'col', split_axis=0, concat_axis=0, tiled=True)]
    all_to_all x1 -> x2, starting transfers between devices: 4.77 us -> 18.7 us  [gather_col(): lax.all_to_all(spread, 'col', split_axis=0, concat_axis=0, tiled=True)]
    div x0 -> x1, other arithmetic: none -> 11.6 us  [local(): 1.0 / (1.0 + jnp.abs(positions[:, :, None] - positions[:, None, :]) / scr...]
    dot_general x2 -> x4, matrix products: 28.2 us -> 33.7 us  [the longest x2 26.4 us: local(): jnp.einsum('pq,qn->pn', mixed_kernel, basis_rows[spin], preferred_element...]
    slice x0 -> x3, local copies, waits for them, and re-layouts: none -> 5.15 us  [local(): basis_rows[spin]]
    transpose x2 -> x1, local copies, waits for them, and re-layouts: 6.8 us -> 1.87 us  [local(): orbitals_all[:, :, 0].transpose(1, 0, 2, 3).reshape(points, slots)]
    all_gather x1, waiting for transfers between devices: 60.7 us -> 65.6 us  [local(): basis_cols = lax.all_gather(own_cols, 'row', axis=1, tiled=True)]
  transfers between devices with their start and end apart: 4 -> 5, of which waited for: 3 -> 4; matrix products, arithmetic and copies ran while one was open for 11% -> 17% of each run, Pallas kernels for 0% -> 0%
where the time goes in v11:
time: 301 us
  waiting for transfers between devices  145 us (48%)
  blocking collectives  51 us (17%)
  matrix products  35.2 us (12%)
  starting transfers between devices  24.3 us (8%)
  local copies, waits for them, and re-layouts  18.2 us (6%)
  between operations  13.6 us (5%)
  other arithmetic  13 us (4%)
    all_gather x1, waiting for transfers between devices, local(): basis_cols = lax.all_gather(own_cols, 'row', axis=1, tiled=True)  65.6 us
    all_to_all x2, waiting for transfers between devices, gather_col(): lax.all_to_all(spread, 'col', split_axis=0, concat_axis=0, tiled=True)  61.4 us
    all_to_all x1, blocking collectives, local(): lax.all_to_all(send, 'row', split_axis=0, concat_axis=0, tiled=True)  28.1 us
    dot_general x2, matrix products, local(): jnp.einsum('pq,qn->pn', mixed_kernel, basis_rows[spin], preferred_element...  26.4 us
    all_to_all x1, blocking collectives, local(): lax.all_to_all(spread, 'row', split_axis=0, concat_axis=0, tiled=True)  22.9 us
    all_to_all x2, starting transfers between devices, gather_col(): lax.all_to_all(spread, 'col', split_axis=0, concat_axis=0, tiled=True)  18.7 us
    all_to_all x1, waiting for transfers between devices, local(): lax.all_to_all(partial_value.astype(jnp.bfloat16), 'row', split_axis=0, c...  18.1 us
    div x1, other arithmetic, local(): 1.0 / (1.0 + jnp.abs(positions[:, :, None] - positions[:, None, :]) / scr...  11.6 us
  transfers between devices with their start and end apart: 5, of which 4 were waited for; matrix products, arithmetic and copies ran while one was open for 17% of the time, Pallas kernels for 0%

profile of v11, /device:TPU:1, one launch (start us, length us, event | category | flops | bytes accessed | tf_op | source)
XLA Modules:
  0.0 300.6 jit_solution(4201878697555818744)
XLA Ops:
  6.5 1.7 copy-done
  9.0 28.1 %all_to_all.25 = bf16[32,2,8,288]{3,2,1,0:T(8,128)(2,1)S(1)} all-to-all(bf16[32,2,8,288]{3,2,1,0:T(8,128)(2,1)S(1)} %copy.9), channel_id=1, replica_groups=mesh['row'=32,'col'=8] {'row'}, dimensions={0} | all-to-all | bytes 589824 | tf_op jit(solution)/shard_map/all_to_all | solution.py:38
  37.1 1.5 fusion.14
  39.5 5.6 %all-to-all-start.1 = ((bf16[32,2,8,512]{3,2,1,0:T(8,128)(2,1)}), bf16[32,2,8,512]{3,2,1,0:T(8,128)(2,1)S(1)}, u32[]{:S(2)}, u32[]{:S(2)}) async-start(bf16[32,2,8,512]{3,2,1,0:T(8,128)(2,1)} %copy.11), calls=%async_computation.1 | async-start | bytes 1048576 | tf_op jit(solution)/shard_map/all_to_all | solution.py:45
  45.2 18.1 %all-to-all-done.1 = bf16[32,2,8,512]{3,2,1,0:T(8,128)(2,1)S(1)} async-done(((bf16[32,2,8,512]{3,2,1,0:T(8,128)(2,1)}), bf16[32,2,8,512]{3,2,1,0:T(8,128)(2,1)S(1)}, u32[]{:S(2)}, u32[]{:S(2)}) %all-to-all-start.1) | async-done | bytes 524320 | tf_op jit(solution)/shard_map/all_to_all | solution.py:45
  63.4 22.9 %all_to_all.26 = bf16[32,2,8,512]{3,2,1,0:T(8,128)(2,1)S(1)} all-to-all(bf16[32,2,8,512]{3,2,1,0:T(8,128)(2,1)S(1)} %broadcast_in_dim.68), channel_id=1, replica_groups=mesh['row'=32,'col'=8] {'row'}, dimensions={0} | all-to-all | bytes 1048576 | tf_op jit(solution)/shard_map/all_to_all | solution.py:52
  88.0 2.1 broadcast_in_dim.71
  90.1 4.6 %all-to-all-start.4 = ((bf16[8,32,2,8,288]{4,3,1,2,0:T(8,128)(2,1)}), bf16[8,32,2,8,288]{4,3,1,2,0:T(8,128)(2,1)}, u32[]{:S(2)}, u32[]{:S(2)}) async-start(bf16[8,32,2,8,288]{4,3,1,2,0:T(8,128)(2,1)} %broadcast_in_dim.71), calls=%async_computation.4 | async-start | bytes 6291456 | tf_op jit(solution)/shard_map/all_to_all | solution.py:16
  95.0 51.1 %all-to-all-done.4 = bf16[8,32,2,8,288]{4,3,1,2,0:T(8,128)(2,1)} async-done(((bf16[8,32,2,8,288]{4,3,1,2,0:T(8,128)(2,1)}), bf16[8,32,2,8,288]{4,3,1,2,0:T(8,128)(2,1)}, u32[]{:S(2)}, u32[]{:S(2)}) %all-to-all-start.4) | async-done | bytes 2359328 | tf_op jit(solution)/shard_map/all_to_all | solution.py:16
  146.0 1.5 broadcast_in_dim.70
  147.5 14.1 %all-to-all-start.3 = ((bf16[8,32,1,8,512]{4,3,1,2,0:T(8,128)(2,1)}), bf16[8,32,1,8,512]{4,3,1,2,0:T(8,128)(2,1)S(1)}, u32[]{:S(2)}, u32[]{:S(2)}) async-start(bf16[8,32,1,8,512]{4,3,1,2,0:T(8,128)(2,1)} %broadcast_in_dim.70), calls=%async_computation.3 | async-start | bytes 4194304 | tf_op jit(solution)/shard_map/all_to_all | solution.py:16
  161.6 11.6 %add_divide_fusion = f32[2,2048,2048]{2,1,0:T(8,128)} fusion(f32[2,2048]{1,0:T(2,128)S(1)} %add_convert_fusion), kind=kLoop, calls=%fused_computation | loop fusion | flops 41943040 | bytes 33570816 | tf_op jit(solution)/shard_map/div | solution.py:57
  173.2 2.2 fusion.27
  175.4 1.4 copy.14
  176.9 1.5 copy.16
  178.3 10.4 %all-to-all-done.3 = bf16[8,32,1,8,512]{4,3,1,2,0:T(8,128)(2,1)S(1)} async-done(((bf16[8,32,1,8,512]{4,3,1,2,0:T(8,128)(2,1)}), bf16[8,32,1,8,512]{4,3,1,2,0:T(8,128)(2,1)S(1)}, u32[]{:S(2)}, u32[]{:S(2)}) %all-to-all-start.3) | async-done | bytes 2097184 | tf_op jit(solution)/shard_map/all_to_all | solution.py:16
  188.7 1.6 copy.12
  190.3 14.5 %convolution_convert_fusion.1 = bf16[2048,288]{0,1:T(8,128)(2,1)S(1)} fusion(bf16[2048,288]{1,0:T(8,128)(2,1)} %bitcast.76, f32[2,2048,2048]{2,1,0:T(8,128)} %add_divide_fusion, bf16[2048,512]{1,0:T(8,128)(2,1)} %bitcast.74), kind=kOutput, calls=%fused_computation.18 | convolution fusion | flops 6724059136 | bytes 23724032 | tf_op jit(solution)/shard_map/pq,qn->pn/dot_general | solution.py:65
  204.9 1.9 copy.15
  206.8 11.9 %convolution_convert_fusion = bf16[2048,288]{0,1:T(8,128)(2,1)} fusion(bf16[2048,288]{1,0:T(8,128)(2,1)} %bitcast.75, f32[2,2048,2048]{2,1,0:T(8,128)} %add_divide_fusion, bf16[2048,512]{1,0:T(8,128)(2,1)S(1)} %bitcast.73), kind=kOutput, calls=%fused_computation.17 | convolution fusion | flops 6724059136 | bytes 23724032 | tf_op jit(solution)/shard_map/pq,qn->pn/dot_general | solution.py:65
  218.7 65.6 %all-gather.4.cloned.1.call-done = bf16[2,2048,1152]{2,1,0:T(8,128)(2,1)} async-done(((bf16[2,64,1152]{2,1,0:T(8,128)(2,1)}), bf16[2,2048,1152]{2,1,0:T(8,128)(2,1)}) %all-gather.4.cloned.1.call-update) | async-done | bytes 9437200 | tf_op jit(solution)/shard_map/all_gather | solution.py:34
  284.3 4.2 %fusion.12 = bf16[1152,1,288]{0,2,1:T(8,128)(2,1)S(1)} fusion(bf16[2048,288]{0,1:T(8,128)(2,1)S(1)} %convolution_convert_fusion.1, bf16[2,2048,1152]{2,1,0:T(8,128)(2,1)} %all-gather.4.cloned.1.call-done), kind=kOutput, calls=%fused_computation.19 | convolution fusion | flops 1359618048 | bytes 6561792 | tf_op jit(solution)/shard_map/pm,pn->mn/dot_general | solution.py:70
  289.4 3.1 %fusion.13 = bf16[1152,1,288]{0,2,1:T(8,128)(2,1)S(1)} fusion(bf16[2048,288]{0,1:T(8,128)(2,1)} %convolution_convert_fusion, bf16[2,2048,1152]{2,1,0:T(8,128)(2,1)S(1)} %copy-done.4), kind=kOutput, calls=%fused_computation.20 | convolution fusion | flops 1359618048 | bytes 6561792 | tf_op jit(solution)/shard_map/pm,pn->mn/dot_general | solution.py:70
  292.5 1.2 pad_maximum_fusion
  (29 shorter events, 4.7 us)
Async XLA Ops:
  6.5 1.7 copy-start
  9.0 36.1 %copy-start.3 = (s32[2]{0:T(128)S(1)}, s32[2]{0:T(128)}, u32[]{:S(2)}) copy-start(s32[2]{0:T(128)} %param.6) | copy-start | bytes 28
  39.5 23.8 %all-to-all-start.1 = ((bf16[32,2,8,512]{3,2,1,0:T(8,128)(2,1)}), bf16[32,2,8,512]{3,2,1,0:T(8,128)(2,1)S(1)}, u32[]{:S(2)}, u32[]{:S(2)}) async-start(bf16[32,2,8,512]{3,2,1,0:T(8,128)(2,1)} %copy.11), calls=%async_computation.1 | async-start | bytes 1048576 | tf_op jit(solution)/shard_map/all_to_all | solution.py:45
  45.0 159.8 %all-gather.6.cloned.1.call-start = ((), (), s32[]{:S(2)}) async-start(), calls=%async_computation.6 | async-start | bytes 2359296 | tf_op jit(solution)/shard_map/all_gather | solution.py:54
  87.1 197.2 %all-gather.4.cloned.1.call-start = ((), (), s32[]{:S(2)}) async-start(), calls=%async_computation.5 | async-start | bytes 9732096 | tf_op jit(solution)/shard_map/all_gather | solution.py:34
  90.1 4.6 %copy-start.2 = (s32[2,2]{1,0:T(2,128)S(1)}, s32[2,2]{1,0:T(2,128)}, u32[]{:S(2)}) copy-start(s32[2,2]{1,0:T(2,128)} %param.7) | copy-start | bytes 52
  90.1 55.9 %all-to-all-start.4 = ((bf16[8,32,2,8,288]{4,3,1,2,0:T(8,128)(2,1)}), bf16[8,32,2,8,288]{4,3,1,2,0:T(8,128)(2,1)}, u32[]{:S(2)}, u32[]{:S(2)}) async-start(bf16[8,32,2,8,288]{4,3,1,2,0:T(8,128)(2,1)} %broadcast_in_dim.71), calls=%async_computation.4 | async-start | bytes 6291456 | tf_op jit(solution)/shard_map/all_to_all | solution.py:16
  147.5 41.2 %all-to-all-start.3 = ((bf16[8,32,1,8,512]{4,3,1,2,0:T(8,128)(2,1)}), bf16[8,32,1,8,512]{4,3,1,2,0:T(8,128)(2,1)S(1)}, u32[]{:S(2)}, u32[]{:S(2)}) async-start(bf16[8,32,1,8,512]{4,3,1,2,0:T(8,128)(2,1)} %broadcast_in_dim.70), calls=%async_computation.3 | async-start | bytes 4194304 | tf_op jit(solution)/shard_map/all_to_all | solution.py:16
  284.3 5.1 %copy-start.4 = (bf16[2,2048,1152]{2,1,0:T(8,128)(2,1)S(1)}, bf16[2,2048,1152]{2,1,0:T(8,128)(2,1)}, u32[]{:S(2)}) copy-start(bf16[2,2048,1152]{2,1,0:T(8,128)(2,1)} %all-gather.4.cloned.1.call-done) | copy-start | bytes 28311556
  289.4 4.3 %copy-start.1 = (bf16[2,64,9216]{2,1,0:T(8,128)(2,1)S(1)}, bf16[2,64,9216]{2,1,0:T(8,128)(2,1)}, u32[]{:S(2)}) copy-start(bf16[2,64,9216]{2,1,0:T(8,128)(2,1)} %param.4) | copy-start | bytes 7077892
Sparse Core Ops, SparseCore 0:
  87.2 76.5 all-gather.5
  166.6 117.6 all-gather.3
